TPU v7x, 256 devices: a whole 4x4x8 slice. The times are simulated.
256 devices in a mesh: seq: 16 (over y, x), chan: 16 (over z, core).
Axes of the slice: x: 4, y: 4, z: 8, core: 2. Of those that a mesh axis runs over, the one named last changes fastest.
Arguments:
- layer_input: bfloat16 [2048, 8192], P('seq', 'chan'), may hold values from -6 to 6
- value_pre: bfloat16 [2048, 8192], P('seq', 'chan'), may hold values from -6 to 6
- gate_act: bfloat16 [2048, 8192], P('seq', 'chan'), may hold values from -6 to 6
- key_act: bfloat16 [2048, 8192], P('seq', 'chan'), may hold values from -6 to 6
- short_taps: float32 [3, 8192], P(None, 'chan'), may hold values from -3 to 3
- long_filter: float32 [2048, 8192], P('seq', 'chan'), may hold values from -0.125 to 0.125
- grad_out: bfloat16 [2048, 8192], P('seq', 'chan'), may hold values from -6 to 6
Outputs:
- grad_gate: bfloat16 [2048, 8192], P('seq', 'chan')
- grad_key: bfloat16 [2048, 8192], P('seq', 'chan')
- grad_value: bfloat16 [2048, 8192], P('seq', 'chan')
- grad_taps: float32 [3, 8192], P(None, 'chan')
- grad_filter: float32 [2048, 8192], P('seq', 'chan')
- grad_proj: float32 [8192, 8192], P('chan', 'seq')
All inputs are finite; a program needn't handle non-finite values.
Results may differ from a plain program's by a relative error of at most 0.0029.
Values may be sent and summed in bfloat16 or wider, within the bound.
No kernel may reach another device: no remote copies, remote signals or barrier semaphores. Data moves between devices by JAX's collectives and lax.ppermute only.
A program may use at most 128 MiB of HBM per device.

v0:
```python
import numpy as np

import jax
import jax.numpy as jnp
from jax import lax
from jax.sharding import PartitionSpec as P

F32 = jnp.float32
BF16 = jnp.bfloat16
PRECISE = lax.Precision.HIGHEST


def angles(rows, cols, period):
    product = np.outer(np.arange(rows), np.arange(cols)) % period
    return product.astype(np.float64) * (2.0 * np.pi / period)


def dft_tables(blocks, width):
    freq_blocks = 2 * blocks
    total = freq_blocks * width
    outer = angles(freq_blocks, blocks, freq_blocks)
    stage_a = np.concatenate([np.cos(outer), -np.sin(outer)], axis=0)
    twist = angles(freq_blocks, width, total)
    twist_cos = np.cos(twist)[:, None, None, :]
    twist_sin = np.sin(twist)[:, None, None, :]
    inner = angles(width, width, width)
    inner_cos, inner_sin = np.cos(inner), np.sin(inner)
    stage_b = np.concatenate(
        [np.concatenate([inner_cos, -inner_sin], axis=1), np.concatenate([inner_sin, inner_cos], axis=1)],
        axis=0,
    )
    back_b = np.concatenate(
        [np.concatenate([inner_cos, inner_sin], axis=1), np.concatenate([-inner_sin, inner_cos], axis=1)],
        axis=0,
    )
    back_a = np.concatenate([np.cos(outer).T, -np.sin(outer).T], axis=1) / total
    as_f32 = lambda a: jnp.asarray(a.astype(np.float32))
    return tuple(as_f32(a) for a in (stage_a, twist_cos, twist_sin, stage_b, back_b, back_a))


def spectra(stacked, tables):
    stage_a, twist_cos, twist_sin, stage_b, _, _ = tables
    freq_blocks = 2 * stacked.shape[0]
    width = stacked.shape[-1]
    outer = jnp.einsum("kp,pscm->kscm", stage_a, stacked, precision=PRECISE)
    outer_re, outer_im = outer[:freq_blocks], outer[freq_blocks:]
    turned_re = outer_re * twist_cos + outer_im * twist_sin
    turned_im = outer_im * twist_cos - outer_re * twist_sin
    spec = jnp.einsum("kscm,mn->kscn", turned_re, stage_b[:width], precision=PRECISE) + jnp.einsum(
        "kscm,mn->kscn", turned_im, stage_b[width:], precision=PRECISE
    )
    return spec[..., :width], spec[..., width:]


def signals_back(prod_re, prod_im, tables):
    _, twist_cos, twist_sin, _, back_b, back_a = tables
    width = prod_re.shape[-1]
    inner = jnp.einsum("kscn,nm->kscm", prod_re, back_b[:width], precision=PRECISE) + jnp.einsum(
        "kscn,nm->kscm", prod_im, back_b[width:], precision=PRECISE
    )
    inner_re, inner_im = inner[..., :width], inner[..., width:]
    back_re = inner_re * twist_cos - inner_im * twist_sin
    back_im = inner_re * twist_sin + inner_im * twist_cos
    both = jnp.concatenate([back_re, back_im], axis=0)
    return jnp.einsum("pk,kscm->pscm", back_a, both, precision=PRECISE)


def shift_back(x, by, lane):
    earlier = jnp.concatenate([jnp.zeros_like(x[:1]), x[:-1]], axis=0)
    return jnp.where(lane < by, jnp.roll(earlier, by, axis=-1), jnp.roll(x, by, axis=-1))


def shift_ahead(x, by, lane):
    later = jnp.concatenate([x[1:], jnp.zeros_like(x[:1])], axis=0)
    width = x.shape[-1]
    return jnp.where(lane >= width - by, jnp.roll(later, -by, axis=-1), jnp.roll(x, -by, axis=-1))


def to_tokens_in_lanes(block, parts):
    rows, cols = block.shape[-2:]
    swapped = jnp.swapaxes(block, -1, -2)
    return swapped.reshape(block.shape[:-2] + (parts, cols // parts, rows))


def from_tokens_in_lanes(block):
    lead = block.shape[:-3]
    parts, sub, rows = block.shape[-3:]
    return jnp.swapaxes(block.reshape(lead + (parts * sub, rows)), -1, -2)


def split_words(x):
    rounded = lax.reduce_precision(x, exponent_bits=8, mantissa_bits=7)
    return rounded.astype(BF16), (x - rounded).astype(BF16)


def join_words(high, low):
    return high.astype(F32) + low.astype(F32)


def on_device(layer_input, value_pre, gate_act, key_act, short_taps, long_filter, grad_out):
    n_seq = lax.axis_size("seq")
    n_chan = lax.axis_size("chan")
    me = lax.axis_index("seq")
    tap_count = short_taps.shape[0]
    sub = value_pre.shape[1] // n_seq

    filt_high, filt_low = split_words(long_filter)
    sent = to_tokens_in_lanes(jnp.stack([value_pre, gate_act, key_act, grad_out, filt_high, filt_low]), n_seq)
    got = lax.all_to_all(sent, "seq", split_axis=1, concat_axis=1, tiled=True)
    value_t = got[0].astype(F32)
    gate_t = got[1].astype(F32)
    key_t = got[2].astype(F32)
    gout_t = got[3].astype(F32)
    filt = join_words(got[4], got[5])
    taps = lax.dynamic_slice_in_dim(short_taps, me * sub, sub, axis=1)[:, :, None]
    lane = lax.broadcasted_iota(jnp.int32, value_t.shape, 2)

    value_shifted = [value_t] + [shift_back(value_t, j, lane) for j in range(1, tap_count)]
    conv_val = taps[0] * value_shifted[0]
    for tap_index in range(1, tap_count):
        conv_val = conv_val + taps[tap_index] * value_shifted[tap_index]
    signal = key_t * conv_val
    grad_mix = gout_t * gate_t
    tables = dft_tables(value_t.shape[0], value_t.shape[2])
    fg_re, fg_im = spectra(jnp.stack([filt, grad_mix], axis=1), tables)
    filt_re, grad_re = fg_re[:, 0:1], fg_re[:, 1:2]
    filt_im, grad_im = fg_im[:, 0:1], fg_im[:, 1:2]
    grad_signal = signals_back(
        filt_re * grad_re + filt_im * grad_im, filt_re * grad_im - filt_im * grad_re, tables
    )[:, 0]
    grad_key = (grad_signal * conv_val).astype(BF16)
    grad_conv = grad_signal * key_t
    value_sum = taps[0] * grad_conv
    for tap_index in range(1, tap_count):
        value_sum = value_sum + taps[tap_index] * shift_ahead(grad_conv, tap_index, lane)
    grad_value = value_sum.astype(BF16)

    swap = [(a * n_chan + b, b * n_chan + a) for a in range(n_seq) for b in range(n_chan)]
    value_swapped = lax.ppermute(grad_value, ("seq", "chan"), swap)
    value_cols = lax.all_gather(value_swapped, "chan", axis=0, tiled=False)
    late_input, _ = lax.optimization_barrier((layer_input, value_swapped))
    inputs_all = lax.all_to_all(
        jnp.broadcast_to(late_input[None], (n_seq,) + late_input.shape),
        "seq", split_axis=0, concat_axis=0, tiled=True,
    ).reshape(-1, late_input.shape[1])

    sig_re, sig_im = spectra(signal[:, None], tables)
    prod_re = jnp.concatenate(
        [filt_re * sig_re - filt_im * sig_im, sig_re * grad_re + sig_im * grad_im], axis=1
    )
    prod_im = jnp.concatenate(
        [filt_re * sig_im + filt_im * sig_re, sig_re * grad_im - sig_im * grad_re], axis=1
    )
    mixed = signals_back(prod_re, prod_im, tables)
    mix_out, grad_filter = mixed[:, 0], mixed[:, 1]
    grad_gate = (gout_t * mix_out).astype(BF16)

    tap_rows = jnp.stack([jnp.sum(grad_conv * value_shifted[j], axis=(0, 2)) for j in range(tap_count)])
    taps_high, taps_low = split_words(tap_rows)
    width = value_t.shape[2]
    taps_slab = jnp.pad(jnp.concatenate([taps_high, taps_low], axis=0).T, ((0, 0), (0, width - 2 * tap_count)))
    taps_slab = jnp.broadcast_to(taps_slab[None], value_t.shape)
    gf_high, gf_low = split_words(grad_filter)
    outs = jnp.stack([grad_gate, grad_key, grad_value, gf_high, gf_low, taps_slab])
    outs = lax.all_to_all(outs, "seq", split_axis=1, concat_axis=1, tiled=True)
    taps_got = outs[5, :, :, : 2 * tap_count]
    grad_taps = join_words(taps_got[..., :tap_count], taps_got[..., tap_count:])
    grad_taps = jnp.transpose(grad_taps, (2, 0, 1)).reshape(tap_count, -1)
    outs = from_tokens_in_lanes(outs[:5])
    grad_filter = join_words(outs[3], outs[4])

    blocks = value_t.shape[0]
    inputs_3 = inputs_all.reshape(blocks, width, inputs_all.shape[1])
    grad_proj = jnp.einsum("pmi,cpom->ico", inputs_3, value_cols, preferred_element_type=F32)
    grad_proj = grad_proj.reshape(grad_proj.shape[0], -1)
    return (outs[0], outs[1], outs[2], grad_taps, grad_filter, grad_proj)


def solution(mesh):
    assert mesh.shape["seq"] == mesh.shape["chan"]
    in_specs = (
        P("seq", "chan"),
        P("seq", "chan"),
        P("seq", "chan"),
        P("seq", "chan"),
        P(None, "chan"),
        P("seq", "chan"),
        P("seq", "chan"),
    )
    out_specs = (
        P("seq", "chan"),
        P("seq", "chan"),
        P("seq", "chan"),
        P(None, "chan"),
        P("seq", "chan"),
        P("chan", "seq"),
    )
    return jax.shard_map(
        on_device, mesh=mesh, in_specs=in_specs, out_specs=out_specs, check_vma=False
    )
```

profile of v0, /device:TPU:1, one launch (start us, length us, event | category | flops | bytes accessed | tf_op | source)
XLA Modules:
  0.0 145.3 jit_solution(13252989115215026495)
XLA Ops:
  7.2 1.1 copy.56
  8.3 1.0 copy.52
  9.3 1.0 copy.53
  10.3 1.0 copy.54
  11.4 1.0 copy.55
  12.6 1.0 copy.58
  13.5 7.6 %all-to-all-start = ((bf16[6,16,32,128]{3,2,0,1:T(8,128)(2,1)}), bf16[6,16,32,128]{3,2,0,1:T(8,128)(2,1)S(1)}, u32[]{:S(2)}, u32[]{:S(2)}) async-start(bf16[6,16,32,128]{3,2,0,1:T(8,128)(2,1)} %copy.58), calls=%async_computation | async-start | bytes 1572864 | tf_op jit(solution)/shard_map/all_to_all | solution.py:109
  21.2 0.1 constant_dynamic-slice_fusion
  21.3 13.1 %all-to-all-done = bf16[6,16,32,128]{3,2,0,1:T(8,128)(2,1)S(1)} async-done(((bf16[6,16,32,128]{3,2,0,1:T(8,128)(2,1)}), bf16[6,16,32,128]{3,2,0,1:T(8,128)(2,1)S(1)}, u32[]{:S(2)}, u32[]{:S(2)}) %all-to-all-start) | async-done | bytes 786464 | tf_op jit(solution)/shard_map/all_to_all | solution.py:109
  34.6 0.1 pad_slice_fusion.5
  34.7 0.1 pad_slice_fusion.7
  34.9 0.1 slice.266
  35.0 0.1 slice.268
  35.2 0.2 fusion.41
  35.3 1.8 %fusion.17 = f32[64,2,32,128]{3,0,2,1:T(8,128)S(1)} fusion(f32[64,16,1,1]{0,1,3,2:T(8,128)S(1)} %copy-done.16, f32[16,1,32,128]{3,0,2,1:T(8,128)S(1)} %get-tuple-element.63, f32[16,1,32,128]{3,0,2,1:T(8,128)S(1)} %get-tuple-element.64), kind=kOutput, calls=%fused_computation.28 | convolution fusion | flops 100794368 | bytes 2625536 | tf_op jit(solution)/shard_map/kp,pscm->kscm/dot_general | solution.py:45
  37.2 0.4 multiply_subtract_fusion.1
  37.6 0.5 copy-done.5
  38.1 2.2 %fusion.15 = f32[32,2,32,256]{3,2,1,0:T(8,128)S(1)} fusion(f32[128,256,1,1]{1,0,3,2:T(8,128)S(1)} %copy-done.5, f32[32,2,32,128]{3,0,2,1:T(8,128)S(1)} %get-tuple-element.41), kind=kOutput, calls=%fused_computation.22 | convolution fusion | flops 805306368 | bytes 3276800 | tf_op jit(solution)/shard_map/kscm,mn->kscn/dot_general | solution.py:49
  40.4 2.2 %convolution_add_fusion.1 = f32[32,2,32,256]{3,2,1,0:T(8,128)S(1)} fusion(f32[32,2,32,256]{3,2,1,0:T(8,128)S(1)} %fusion.15, f32[128,256,1,1]{1,0,3,2:T(8,128)S(1)} %copy-done.12, f32[32,2,32,128]{3,0,2,1:T(8,128)S(1)} %get-tuple-element.40), kind=kOutput, calls=%fused_computation.8 | convolution fusion | flops 805830656 | bytes 5373952 | tf_op jit(solution)/shard_map/kscm,mn->kscn/dot_general | solution.py:49
  42.6 1.0 fusion.22
  43.6 1.0 fusion.7
  44.6 0.1 multiply_subtract_fusion.2
  44.8 0.1 maximum_bitcast_fusion
  44.8 0.5 copy-done.15
  45.3 1.7 %multiply_reduce_fusion.2 = (f32[32]{0:T(128)S(1)}, f32[32]{0:T(128)S(1)}, f32[32]{0:T(128)S(1)}, f32[16,32,128]{2,0,1:T(8,128)S(1)}, f32[16,32,128]{2,0,1:T(8,1...) fusion(bf16[1,16,32,128]{3,2,0,1:T(8,128)(2,1)S(1)} %get-tuple-element.46, ...), kind=kOutput, calls=%fused_computation.89 | convolution fusion | flops 51314592 | bytes 3412608 | tf_op jit(solution)/shard_map/pk,kscm->pscm/dot_general | solution.py:65
  47.1 0.1 pad_slice_fusion.1
  47.3 0.1 pad_slice_fusion.3
  47.4 0.1 slice.283
  47.5 0.1 slice.285
  47.7 1.3 fusion.43
  49.0 0.2 multiply_subtract_fusion.5
  49.2 1.2 fusion.25
  50.4 1.2 fusion.8
  51.5 0.3 multiply_add_fusion.3
  51.9 0.1 pad_maximum_fusion.1
  52.0 0.1 pad_maximum_fusion
  52.1 0.7 copy-done.4
  52.8 2.2 %fusion.10 = f32[32,2,32,256]{3,0,2,1:T(8,128)S(1)} fusion(f32[128,256,1,1]{1,0,3,2:T(8,128)S(1)} %copy-done.4, f32[32,2,32,128]{3,2,1,0:T(8,128)S(1)} %pad_maximum_fusion), kind=kOutput, calls=%fused_computation.17 | convolution fusion | flops 805306368 | bytes 3276800 | tf_op jit(solution)/shard_map/kscn,nm->kscm/dot_general | solution.py:58
  55.0 2.2 %convolution_add_fusion = f32[32,2,32,256]{3,0,2,1:T(8,128)S(1)} fusion(f32[32,2,32,256]{3,0,2,1:T(8,128)S(1)} %fusion.10, f32[128,256,1,1]{1,0,3,2:T(8,128)S(1)} %copy-done.11, f32[32,2,32,128]{3,2,1,0:T(8,128)S(1)} %pad_maximum_fusion.1), kind=kOutput, calls=%fused_computation.7 | convolution fusion | flops 805830656 | bytes 5373952 | tf_op jit(solution)/shard_map/kscn,nm->kscm/dot_general | solution.py:58
  57.3 0.2 multiply_subtract_fusion
  57.5 0.5 copy-done.13
  57.9 1.1 fusion
  59.1 0.2 fusion.52
  59.3 0.5 bitcast_dynamic-update-slice_fusion
  59.8 4.1 %collective-permute-start = (bf16[16,32,128]{2,0,1:T(8,128)(2,1)S(1)}, bf16[16,32,128]{2,0,1:T(8,128)(2,1)S(1)}, u32[]{:S(2)}, u32[]{:S(2)}) collective-permute-start(bf16[16,32,128]{2,0,1:T(8,128)(2,1)S(1)} %get-tuple-element.33), channel_id=1, source_target_pairs={{0,0},{1,16},{2,32},{3,48},{4,64},{5,80},{6,96},{7,112},{8,128},{9... | collective-permute-start | bytes 393224 | tf_op jit(solution)/shard_map/ppermute | solution.py:139
  64.0 3.8 %collective-permute-done = bf16[16,32,128]{2,0,1:T(8,128)(2,1)S(1)} collective-permute-done((bf16[16,32,128]{2,0,1:T(8,128)(2,1)S(1)}, bf16[16,32,128]{2,0,1:T(8,128)(2,1)S(1)}, u32[]{:S(2)}, u32[]{:S(2)}) %collective-permute-start) | collective-permute-done | bytes 131104 | tf_op jit(solution)/shard_map/ppermute | solution.py:139
  67.7 0.6 copy-done.6
  68.4 0.1 copy.101
  68.7 1.1 copy.73
  69.8 18.2 %all-to-all-start.1 = ((bf16[6,16,32,128]{3,2,0,1:T(8,128)(2,1)}), bf16[6,16,32,128]{3,2,0,1:T(8,128)(2,1)S(1)}, u32[]{:S(2)}, u32[]{:S(2)}) async-start(bf16[6,16,32,128]{3,2,0,1:T(8,128)(2,1)} %copy.73), calls=%async_computation.1 | async-start | bytes 1572864 | tf_op jit(solution)/shard_map/all_to_all | solution.py:165
  88.0 13.0 %all-to-all-done.1 = bf16[6,16,32,128]{3,2,0,1:T(8,128)(2,1)S(1)} async-done(((bf16[6,16,32,128]{3,2,0,1:T(8,128)(2,1)}), bf16[6,16,32,128]{3,2,0,1:T(8,128)(2,1)S(1)}, u32[]{:S(2)}, u32[]{:S(2)}) %all-to-all-start.1) | async-done | bytes 786464 | tf_op jit(solution)/shard_map/all_to_all | solution.py:165
  101.0 1.5 %broadcast_in_dim.2 = bf16[16,128,512]{2,1,0:T(8,128)(2,1)} broadcast(bf16[128,512]{1,0:T(8,128)(2,1)S(1)} %copy-done.3), dimensions={1,2} | broadcast | bytes 2228224 | tf_op jit(solution)/shard_map/broadcast_in_dim | solution.py:143
  102.5 4.1 %all-to-all-start.2 = ((bf16[16,128,512]{2,1,0:T(8,128)(2,1)}), bf16[16,128,512]{2,1,0:T(8,128)(2,1)S(1)}, u32[]{:S(2)}, u32[]{:S(2)}) async-start(bf16[16,128,512]{2,1,0:T(8,128)(2,1)} %broadcast_in_dim.2), calls=%async_computation.2 | async-start | bytes 4194304 | tf_op jit(solution)/shard_map/all_to_all | solution.py:142
  106.7 0.8 slice_bitcast_fusion.4
  107.5 1.7 %copy.77 = bf16[128,512]{1,0:T(8,128)(2,1)} copy(bf16[128,512]{0,1:T(8,128)(2,1)} %get-tuple-element.54) | data formatting | bytes 262144
  109.2 1.7 %copy.78 = bf16[128,512]{1,0:T(8,128)(2,1)} copy(bf16[128,512]{0,1:T(8,128)(2,1)} %get-tuple-element.53) | data formatting | bytes 262144
  110.8 1.7 %copy.79 = bf16[128,512]{1,0:T(8,128)(2,1)} copy(bf16[128,512]{0,1:T(8,128)(2,1)} %get-tuple-element.52) | data formatting | bytes 262144
  112.5 0.7 add_bitcast_fusion
  113.2 1.8 %copy.80 = f32[128,512]{1,0:T(8,128)} copy(f32[128,512]{0,1:T(8,128)} %add_bitcast_fusion) | data formatting | bytes 524288
  115.0 0.1 convert_add_fusion
  115.1 0.7 copy.93
  115.8 18.3 %all-to-all-done.2 = bf16[16,128,512]{2,1,0:T(8,128)(2,1)S(1)} async-done(((bf16[16,128,512]{2,1,0:T(8,128)(2,1)}), bf16[16,128,512]{2,1,0:T(8,128)(2,1)S(1)}, u32[]{:S(2)}, u32[]{:S(2)}) %all-to-all-start.2) | async-done | bytes 2097184 | tf_op jit(solution)/shard_map/all_to_all | solution.py:142
  134.2 3.0 %fusion.4 = f32[512,16,32,1]{0,2,3,1:T(8,128)S(1)} fusion(bf16[16,128,512]{2,1,0:T(8,128)(2,1)S(1)} %all-to-all-done.2, bf16[16,16,32,128]{3,1,0,2:T(8,128)(2,1)} %bitcast.166), kind=kOutput, calls=%fused_computation.4 | convolution fusion | flops 1073741824 | bytes 5242880 | tf_op jit(solution)/shard_map/pmi,cpom->ico/dot_general | solution.py:174
  137.1 1.3 copy.81
  (59 shorter events, 0.9 us)
Async XLA Ops:
  7.2 14.0 %copy-start = (f32[3,512]{1,0:T(4,128)S(1)}, f32[3,512]{1,0:T(4,128)}, u32[]{:S(2)}) copy-start(f32[3,512]{1,0:T(4,128)} %param.17) | copy-start | bytes 18436
  13.5 20.8 %all-to-all-start = ((bf16[6,16,32,128]{3,2,0,1:T(8,128)(2,1)}), bf16[6,16,32,128]{3,2,0,1:T(8,128)(2,1)S(1)}, u32[]{:S(2)}, u32[]{:S(2)}) async-start(bf16[6,16,32,128]{3,2,0,1:T(8,128)(2,1)} %copy.58), calls=%async_computation | async-start | bytes 1572864 | tf_op jit(solution)/shard_map/all_to_all | solution.py:109
  21.1 113.0 %all-gather.3.cloned.1.call-start = ((), (), s32[]{:S(2)}) async-start(), calls=%async_computation.3 | async-start | bytes 2228224 | tf_op jit(solution)/shard_map/all_gather | solution.py:140
  34.5 0.8 copy-start.16
  35.0 2.2 %copy-start.1 = (f32[32,128]{1,0:T(8,128)S(1)}, f32[32,128]{1,0:T(8,128)}, u32[]{:S(2)}) copy-start(f32[32,128]{1,0:T(8,128)} %constant.48) | copy-start | bytes 49156
  35.0 2.2 %copy-start.2 = (f32[32,128]{1,0:T(8,128)S(1)}, f32[32,128]{1,0:T(8,128)}, u32[]{:S(2)}) copy-start(f32[32,128]{1,0:T(8,128)} %constant.49) | copy-start | bytes 49156
  37.2 0.9 copy-start.5
  37.6 2.8 %copy-start.12 = (f32[128,256,1,1]{1,0,3,2:T(8,128)S(1)}, f32[128,256,1,1]{1,0,3,2:T(8,128)}, u32[]{:S(2)}) copy-start(f32[128,256,1,1]{1,0,3,2:T(8,128)} %constant.57) | copy-start | bytes 393220
  40.4 2.3 %copy-start.8 = (f32[128,256,1]{1,0,2:T(8,128)S(1)}, f32[128,256,1]{1,0,2:T(8,128)}, u32[]{:S(2)}) copy-start(f32[128,256,1]{1,0,2:T(8,128)} %constant.64) | copy-start | bytes 393220
  40.4 3.3 %copy-start.10 = (f32[128,256,1]{1,0,2:T(8,128)S(1)}, f32[128,256,1]{1,0,2:T(8,128)}, u32[]{:S(2)}) copy-start(f32[128,256,1]{1,0,2:T(8,128)} %constant.65) | copy-start | bytes 393220
  44.6 0.7 copy-start.15
  47.0 0.7 copy-start.14
  47.7 1.5 %copy-start.7 = (f32[128,256,1]{1,0,2:T(8,128)S(1)}, f32[128,256,1]{1,0,2:T(8,128)}, u32[]{:S(2)}) copy-start(f32[128,256,1]{1,0,2:T(8,128)} %constant.59) | copy-start | bytes 393220
  49.0 1.3 copy-start.9
  51.9 0.9 copy-start.4
  52.8 2.2 %copy-start.11 = (f32[128,256,1,1]{1,0,3,2:T(8,128)S(1)}, f32[128,256,1,1]{1,0,3,2:T(8,128)}, u32[]{:S(2)}) copy-start(f32[128,256,1,1]{1,0,3,2:T(8,128)} %constant.62) | copy-start | bytes 393220
  57.2 0.7 copy-start.13
  59.8 7.9 %collective-permute-start = (bf16[16,32,128]{2,0,1:T(8,128)(2,1)S(1)}, bf16[16,32,128]{2,0,1:T(8,128)(2,1)S(1)}, u32[]{:S(2)}, u32[]{:S(2)}) collective-permute-start(bf16[16,32,128]{2,0,1:T(8,128)(2,1)S(1)} %get-tuple-element.33), channel_id=1, source_target_pairs={{0,0},{1,16},{2,32},{3,48},{4,64},{5,80},{6,96},{7,112},{8,128},{9... | collective-permute-start | bytes 393224 | tf_op jit(solution)/shard_map/ppermute | solution.py:139
  67.7 0.7 copy-start.6
  67.7 33.2 %copy-start.3 = (bf16[128,512]{1,0:T(8,128)(2,1)S(1)}, bf16[128,512]{1,0:T(8,128)(2,1)}, u32[]{:S(2)}) copy-start(bf16[128,512]{1,0:T(8,128)(2,1)} %param.13) | copy-start | bytes 393220
  69.8 31.2 %all-to-all-start.1 = ((bf16[6,16,32,128]{3,2,0,1:T(8,128)(2,1)}), bf16[6,16,32,128]{3,2,0,1:T(8,128)(2,1)S(1)}, u32[]{:S(2)}, u32[]{:S(2)}) async-start(bf16[6,16,32,128]{3,2,0,1:T(8,128)(2,1)} %copy.73), calls=%async_computation.1 | async-start | bytes 1572864 | tf_op jit(solution)/shard_map/all_to_all | solution.py:165
  102.5 31.7 %all-to-all-start.2 = ((bf16[16,128,512]{2,1,0:T(8,128)(2,1)}), bf16[16,128,512]{2,1,0:T(8,128)(2,1)S(1)}, u32[]{:S(2)}, u32[]{:S(2)}) async-start(bf16[16,128,512]{2,1,0:T(8,128)(2,1)} %broadcast_in_dim.2), calls=%async_computation.2 | async-start | bytes 4194304 | tf_op jit(solution)/shard_map/all_to_all | solution.py:142
Sparse Core Ops, SparseCore 0:
  68.5 52.7 all-gather.2
where the time goes:
time: 147 us; the launch traced here: 145 us
  waiting for transfers between devices  48.2 us (33%)
  starting transfers between devices  34.1 us (23%)
  local copies, waits for them, and re-layouts  22.9 us (16%)
  matrix products  22 us (15%)
  between operations  14.7 us (10%)
  other arithmetic  3.45 us (2%)
    all_to_all x1, waiting for transfers between devices, on_device(): lax.all_to_all(jnp.broadcast_to(late_input[None], (n_seq,) + late_input.s...  18.3 us
    all_to_all x1, starting transfers between devices, on_device(): outs = lax.all_to_all(outs, 'seq', split_axis=1, concat_axis=1, tiled=True)  18.2 us
    unnamed x50, local copies, waits for them, and re-layouts  16.4 us
    all_to_all x1, waiting for transfers between devices, on_device(): got = lax.all_to_all(sent, 'seq', split_axis=1, concat_axis=1, tiled=True)  13.1 us
    all_to_all x1, waiting for transfers between devices, on_device(): outs = lax.all_to_all(outs, 'seq', split_axis=1, concat_axis=1, tiled=True)  13 us
    all_to_all x1, starting transfers between devices, on_device(): got = lax.all_to_all(sent, 'seq', split_axis=1, concat_axis=1, tiled=True)  7.57 us
    ppermute x1, starting transfers between devices, on_device(): value_swapped = lax.ppermute(grad_value, ('seq', 'chan'), swap)  4.14 us
    all_to_all x1, starting transfers between devices, on_device(): lax.all_to_all(jnp.broadcast_to(late_input[None], (n_seq,) + late_input.s...  4.12 us
  transfers between devices with their start and end apart: 5, of which 4 were waited for; matrix products, arithmetic and copies ran while one was open for 8% of the time, Pallas kernels for 0%

commit v1 on v0

--- a/solution.py
+++ b/solution.py
@@ -104,6 +104,8 @@
     tap_count = short_taps.shape[0]
     sub = value_pre.shape[1] // n_seq
 
+    inputs_all = lax.all_gather(layer_input, "seq", axis=0, tiled=True)
+
     filt_high, filt_low = split_words(long_filter)
     sent = to_tokens_in_lanes(jnp.stack([value_pre, gate_act, key_act, grad_out, filt_high, filt_low]), n_seq)
     got = lax.all_to_all(sent, "seq", split_axis=1, concat_axis=1, tiled=True)
@@ -138,11 +140,6 @@
     swap = [(a * n_chan + b, b * n_chan + a) for a in range(n_seq) for b in range(n_chan)]
     value_swapped = lax.ppermute(grad_value, ("seq", "chan"), swap)
     value_cols = lax.all_gather(value_swapped, "chan", axis=0, tiled=False)
-    late_input, _ = lax.optimization_barrier((layer_input, value_swapped))
-    inputs_all = lax.all_to_all(
-        jnp.broadcast_to(late_input[None], (n_seq,) + late_input.shape),
-        "seq", split_axis=0, concat_axis=0, tiled=True,
-    ).reshape(-1, late_input.shape[1])
 
     sig_re, sig_im = spectra(signal[:, None], tables)
     prod_re = jnp.concatenate(

time: 147 us -> 143 us (0.973)
  starting transfers between devices: 34.1 us -> 11.8 us
  blocking collectives: 0 us -> 19.7 us
  local copies, waits for them, and re-layouts: 22.9 us -> 16.2 us
  waiting for transfers between devices: 48.2 us -> 54.2 us
    all_to_all x2 -> x0, waiting for transfers between devices: 31.3 us -> none  [the longest x1 18.3 us: on_device(): lax.all_to_all(jnp.broadcast_to(late_input[None], (n_seq,) + late_input.s...]
    all_gather x1, waiting for transfers between devices: 0.01 us -> 25.7 us  [on_device(): value_cols = lax.all_gather(value_swapped, 'chan', axis=0, tiled=False)]
    all_to_all x2 -> x0, starting transfers between devices: 22.3 us -> none  [the longest x1 18.2 us: on_device(): outs = lax.all_to_all(outs, 'seq', split_axis=1, concat_axis=1, tiled=True)]
    all_to_all x0 -> x1, blocking collectives: none -> 19.7 us  [on_device(): outs = lax.all_to_all(outs, 'seq', split_axis=1, concat_axis=1, tiled=True)]
    ppermute x1, waiting for transfers between devices: 3.77 us -> 15.5 us  [on_device(): value_swapped = lax.ppermute(grad_value, ('seq', 'chan'), swap)]
    unnamed x50 -> x48, local copies, waits for them, and re-layouts: 16.4 us -> 12.9 us
    broadcast_in_dim x1 -> x0, local copies, waits for them, and re-layouts: 1.52 us -> none  [on_device(): jnp.broadcast_to(late_input[None], (n_seq,) + late_input.shape)]
  transfers between devices with their start and end apart: 5 -> 4, of which waited for: 4 -> 3; matrix products, arithmetic and copies ran while one was open for 8% -> 19% of each run, Pallas kernels for 0% -> 0%
where the time goes in v1:
time: 143 us; the launch traced here: 142 us
  waiting for transfers between devices  54.2 us (38%)
  matrix products  22.8 us (16%)
  blocking collectives  19.7 us (14%)
  local copies, waits for them, and re-layouts  16.2 us (11%)
  between operations  14.7 us (10%)
  starting transfers between devices  11.8 us (8%)
  other arithmetic  2.64 us (2%)
    all_gather x1, waiting for transfers between devices, on_device(): value_cols = lax.all_gather(value_swapped, 'chan', axis=0, tiled=False)  25.7 us
    all_to_all x1, blocking collectives, on_device(): outs = lax.all_to_all(outs, 'seq', split_axis=1, concat_axis=1, tiled=True)  19.7 us
    ppermute x1, waiting for transfers between devices, on_device(): value_swapped = lax.ppermute(grad_value, ('seq', 'chan'), swap)  15.5 us
    unnamed x48, local copies, waits for them, and re-layouts  12.9 us
    all_to_all x1, waiting for transfers between devices, on_device(): got = lax.all_to_all(sent, 'seq', split_axis=1, concat_axis=1, tiled=True)  12.3 us
    all_to_all x1, starting transfers between devices, on_device(): got = lax.all_to_all(sent, 'seq', split_axis=1, concat_axis=1, tiled=True)  7.57 us
    ppermute x1, starting transfers between devices, on_device(): value_swapped = lax.ppermute(grad_value, ('seq', 'chan'), swap)  4.15 us
    dot_general x1, matrix products, on_device(): jnp.einsum('pmi,cpom->ico', inputs_3, value_cols, preferred_element_type=...  3.58 us
  transfers between devices with their start and end apart: 4, of which 3 were waited for; matrix products, arithmetic and copies ran while one was open for 19% of the time, Pallas kernels for 0%

profile of v1, /device:TPU:1, one launch (start us, length us, event | category | flops | bytes accessed | tf_op | source)
XLA Modules:
  0.0 142.0 jit_solution(13228594586491211549)
XLA Ops:
  7.2 1.0 copy.52
  8.2 1.0 copy.53
  9.3 1.0 copy.54
  10.3 1.0 copy.55
  11.3 1.1 copy.56
  12.6 1.0 copy.58
  13.5 7.6 %all-to-all-start = ((bf16[6,16,32,128]{3,2,0,1:T(8,128)(2,1)}), bf16[6,16,32,128]{3,2,0,1:T(8,128)(2,1)S(1)}, u32[]{:S(2)}, u32[]{:S(2)}) async-start(bf16[6,16,32,128]{3,2,0,1:T(8,128)(2,1)} %copy.58), calls=%async_computation | async-start | bytes 1572864 | tf_op jit(solution)/shard_map/all_to_all | solution.py:111
  21.2 0.7 all-gather.4.cloned.1.call-update
  21.9 0.1 constant_dynamic-slice_fusion
  22.0 12.3 %all-to-all-done = bf16[6,16,32,128]{3,2,0,1:T(8,128)(2,1)S(1)} async-done(((bf16[6,16,32,128]{3,2,0,1:T(8,128)(2,1)}), bf16[6,16,32,128]{3,2,0,1:T(8,128)(2,1)S(1)}, u32[]{:S(2)}, u32[]{:S(2)}) %all-to-all-start) | async-done | bytes 786464 | tf_op jit(solution)/shard_map/all_to_all | solution.py:111
  34.3 0.1 fusion.64
  34.6 0.1 pad_slice_fusion.7
  34.7 0.1 slice.266
  34.8 0.1 slice.268
  35.0 0.1 pad_slice_fusion.5
  35.2 0.2 fusion.40
  35.3 1.8 %fusion.16 = f32[64,2,32,128]{3,0,2,1:T(8,128)S(1)} fusion(f32[64,16,1,1]{0,1,3,2:T(8,128)S(1)} %copy-done.15, f32[16,1,32,128]{3,0,2,1:T(8,128)S(1)} %get-tuple-element.61, f32[16,1,32,128]{3,0,2,1:T(8,128)S(1)} %get-tuple-element.62), kind=kOutput, calls=%fused_computation.27 | convolution fusion | flops 100794368 | bytes 2625536 | tf_op jit(solution)/shard_map/kp,pscm->kscm/dot_general | solution.py:45
  37.2 0.3 multiply_subtract_fusion.1
  37.5 0.6 copy-done.4
  38.1 2.3 %fusion.14 = f32[32,2,32,256]{3,2,1,0:T(8,128)S(1)} fusion(f32[128,256,1,1]{1,0,3,2:T(8,128)S(1)} %copy-done.4, f32[32,2,32,128]{3,0,2,1:T(8,128)S(1)} %get-tuple-element.39), kind=kOutput, calls=%fused_computation.21 | convolution fusion | flops 805306368 | bytes 3276800 | tf_op jit(solution)/shard_map/kscm,mn->kscn/dot_general | solution.py:49
  40.4 2.3 %convolution_add_fusion.1 = f32[32,2,32,256]{3,2,1,0:T(8,128)S(1)} fusion(f32[32,2,32,256]{3,2,1,0:T(8,128)S(1)} %fusion.14, f32[128,256,1,1]{1,0,3,2:T(8,128)S(1)} %copy-done.11, f32[32,2,32,128]{3,0,2,1:T(8,128)S(1)} %get-tuple-element.38), kind=kOutput, calls=%fused_computation.7 | convolution fusion | flops 805830656 | bytes 5373952 | tf_op jit(solution)/shard_map/kscm,mn->kscn/dot_general | solution.py:49
  42.8 1.0 fusion.21
  43.8 1.0 fusion.6
  44.7 0.2 multiply_subtract_fusion.2
  44.9 0.1 maximum_bitcast_fusion
  45.0 0.4 copy-done.14
  45.4 1.7 %multiply_reduce_fusion.2 = (f32[32]{0:T(128)S(1)}, f32[32]{0:T(128)S(1)}, f32[32]{0:T(128)S(1)}, f32[16,32,128]{2,0,1:T(8,128)S(1)}, f32[16,32,128]{2,0,1:T(8,1...) fusion(bf16[1,16,32,128]{3,2,0,1:T(8,128)(2,1)S(1)} %get-tuple-element.44, ...), kind=kOutput, calls=%fused_computation.88 | convolution fusion | flops 51314592 | bytes 3412608 | tf_op jit(solution)/shard_map/pk,kscm->pscm/dot_general | solution.py:65
  47.2 0.1 slice.285
  47.3 0.1 slice.283
  47.5 0.1 pad_slice_fusion.1
  47.7 0.1 pad_slice_fusion.3
  47.8 0.1 copy-done.13
  47.9 1.3 fusion.42
  49.1 0.1 multiply_subtract_fusion.5
  49.3 1.2 fusion.24
  50.5 1.2 fusion.7
  51.6 0.3 multiply_add_fusion.3
  52.0 0.1 pad_maximum_fusion
  52.1 0.1 pad_maximum_fusion.1
  52.2 0.7 copy-done.3
  52.9 2.2 %fusion.9 = f32[32,2,32,256]{3,0,2,1:T(8,128)S(1)} fusion(f32[128,256,1,1]{1,0,3,2:T(8,128)S(1)} %copy-done.3, f32[32,2,32,128]{3,2,1,0:T(8,128)S(1)} %pad_maximum_fusion), kind=kOutput, calls=%fused_computation.16 | convolution fusion | flops 805306368 | bytes 3276800 | tf_op jit(solution)/shard_map/kscn,nm->kscm/dot_general | solution.py:58
  55.1 2.3 %convolution_add_fusion = f32[32,2,32,256]{3,0,2,1:T(8,128)S(1)} fusion(f32[32,2,32,256]{3,0,2,1:T(8,128)S(1)} %fusion.9, f32[128,256,1,1]{1,0,3,2:T(8,128)S(1)} %copy-done.10, f32[32,2,32,128]{3,2,1,0:T(8,128)S(1)} %pad_maximum_fusion.1), kind=kOutput, calls=%fused_computation.6 | convolution fusion | flops 805830656 | bytes 5373952 | tf_op jit(solution)/shard_map/kscn,nm->kscm/dot_general | solution.py:58
  57.4 0.2 multiply_subtract_fusion
  57.7 0.5 copy-done.12
  58.1 1.1 fusion
  59.2 0.1 fusion.55
  59.3 0.2 fusion.51
  59.5 0.5 bitcast_dynamic-update-slice_fusion
  60.0 4.1 %collective-permute-start = (bf16[16,32,128]{2,0,1:T(8,128)(2,1)S(1)}, bf16[16,32,128]{2,0,1:T(8,128)(2,1)S(1)}, u32[]{:S(2)}, u32[]{:S(2)}) collective-permute-start(bf16[16,32,128]{2,0,1:T(8,128)(2,1)S(1)} %get-tuple-element.31), channel_id=1, source_target_pairs={{0,0},{1,16},{2,32},{3,48},{4,64},{5,80},{6,96},{7,112},{8,128},{9... | collective-permute-start | bytes 393224 | tf_op jit(solution)/shard_map/ppermute | solution.py:141
  64.2 15.5 %collective-permute-done = bf16[16,32,128]{2,0,1:T(8,128)(2,1)S(1)} collective-permute-done((bf16[16,32,128]{2,0,1:T(8,128)(2,1)S(1)}, bf16[16,32,128]{2,0,1:T(8,128)(2,1)S(1)}, u32[]{:S(2)}, u32[]{:S(2)}) %collective-permute-start) | collective-permute-done | bytes 131104 | tf_op jit(solution)/shard_map/ppermute | solution.py:141
  79.6 0.7 copy-done.5
  80.3 0.1 copy.101
  80.6 0.2 copy.73
  80.8 19.7 %all_to_all.10 = bf16[6,16,32,128]{3,2,0,1:T(8,128)(2,1)S(1)} all-to-all(bf16[6,16,32,128]{3,2,0,1:T(8,128)(2,1)S(1)} %copy.73), channel_id=1, replica_groups=mesh['seq'=16,'chan'=16] {'seq'}, dimensions={1} | all-to-all | bytes 1572864 | tf_op jit(solution)/shard_map/all_to_all | solution.py:162
  100.5 0.1 copy.100
  100.6 0.8 copy.77
  101.3 0.8 copy.78
  102.1 0.8 copy.79
  102.9 0.1 convert_add_fusion
  103.0 0.7 copy.93
  103.8 0.8 copy.80
  104.6 25.7 %all-gather.6.cloned.1.call-done = bf16[256,32,128]{2,0,1:T(8,128)(2,1)} async-done(((bf16[16,32,128]{2,0,1:T(8,128)(2,1)}), bf16[256,32,128]{2,0,1:T(8,128)(2,1)}) %all-gather.6.cloned.1.call-update) | async-done | bytes 2097168 | tf_op jit(solution)/shard_map/all_gather | solution.py:142
  130.3 3.6 %fusion.4 = f32[16,32,512,1]{2,1,3,0:T(8,128)S(1)} fusion(bf16[16,128,512,1]{2,1,0,3:T(8,128)(2,1)} %bitcast.169, bf16[16,16,32,128]{3,1,0,2:T(8,128)(2,1)} %bitcast.170), kind=kOutput, calls=%fused_computation.4 | convolution fusion | flops 1073741824 | bytes 5242880 | tf_op jit(solution)/shard_map/pmi,cpom->ico/dot_general | solution.py:171
  133.9 1.3 copy.81
  (56 shorter events, 0.8 us)
Async XLA Ops:
  7.2 14.8 %copy-start = (f32[3,512]{1,0:T(4,128)S(1)}, f32[3,512]{1,0:T(4,128)}, u32[]{:S(2)}) copy-start(f32[3,512]{1,0:T(4,128)} %param.17) | copy-start | bytes 18436
  13.5 20.8 %all-to-all-start = ((bf16[6,16,32,128]{3,2,0,1:T(8,128)(2,1)}), bf16[6,16,32,128]{3,2,0,1:T(8,128)(2,1)S(1)}, u32[]{:S(2)}, u32[]{:S(2)}) async-start(bf16[6,16,32,128]{3,2,0,1:T(8,128)(2,1)} %copy.58), calls=%async_computation | async-start | bytes 1572864 | tf_op jit(solution)/shard_map/all_to_all | solution.py:111
  21.1 83.5 %all-gather.4.cloned.1.call-start = ((), (), s32[]{:S(2)}) async-start(), calls=%async_computation.2 | async-start | bytes 2228224 | tf_op jit(solution)/shard_map/all_gather | solution.py:107
  21.9 108.4 %all-gather.6.cloned.1.call-start = ((), (), s32[]{:S(2)}) async-start(), calls=%async_computation.3 | async-start | bytes 2228224 | tf_op jit(solution)/shard_map/all_gather | solution.py:142
  34.5 0.8 copy-start.15
  35.0 2.2 %copy-start.1 = (f32[32,128]{1,0:T(8,128)S(1)}, f32[32,128]{1,0:T(8,128)}, u32[]{:S(2)}) copy-start(f32[32,128]{1,0:T(8,128)} %constant.49) | copy-start | bytes 49156
  35.0 2.2 %copy-start.2 = (f32[32,128]{1,0:T(8,128)S(1)}, f32[32,128]{1,0:T(8,128)}, u32[]{:S(2)}) copy-start(f32[32,128]{1,0:T(8,128)} %constant.48) | copy-start | bytes 49156
  37.2 0.9 copy-start.4
  37.5 2.9 %copy-start.11 = (f32[128,256,1,1]{1,0,3,2:T(8,128)S(1)}, f32[128,256,1,1]{1,0,3,2:T(8,128)}, u32[]{:S(2)}) copy-start(f32[128,256,1,1]{1,0,3,2:T(8,128)} %constant.57) | copy-start | bytes 393220
  40.4 2.3 %copy-start.7 = (f32[128,256,1]{1,0,2:T(8,128)S(1)}, f32[128,256,1]{1,0,2:T(8,128)}, u32[]{:S(2)}) copy-start(f32[128,256,1]{1,0,2:T(8,128)} %constant.64) | copy-start | bytes 393220
  40.4 3.3 %copy-start.9 = (f32[128,256,1]{1,0,2:T(8,128)S(1)}, f32[128,256,1]{1,0,2:T(8,128)}, u32[]{:S(2)}) copy-start(f32[128,256,1]{1,0,2:T(8,128)} %constant.65) | copy-start | bytes 393220
  44.7 0.7 copy-start.14
  47.2 0.7 copy-start.13
  47.8 1.5 %copy-start.6 = (f32[128,256,1]{1,0,2:T(8,128)S(1)}, f32[128,256,1]{1,0,2:T(8,128)}, u32[]{:S(2)}) copy-start(f32[128,256,1]{1,0,2:T(8,128)} %constant.59) | copy-start | bytes 393220
  49.1 1.3 copy-start.8
  52.0 0.9 copy-start.3
  52.9 2.2 %copy-start.10 = (f32[128,256,1,1]{1,0,3,2:T(8,128)S(1)}, f32[128,256,1,1]{1,0,3,2:T(8,128)}, u32[]{:S(2)}) copy-start(f32[128,256,1,1]{1,0,3,2:T(8,128)} %constant.62) | copy-start | bytes 393220
  57.4 0.7 copy-start.12
  60.0 19.6 %collective-permute-start = (bf16[16,32,128]{2,0,1:T(8,128)(2,1)S(1)}, bf16[16,32,128]{2,0,1:T(8,128)(2,1)S(1)}, u32[]{:S(2)}, u32[]{:S(2)}) collective-permute-start(bf16[16,32,128]{2,0,1:T(8,128)(2,1)S(1)} %get-tuple-element.31), channel_id=1, source_target_pairs={{0,0},{1,16},{2,32},{3,48},{4,64},{5,80},{6,96},{7,112},{8,128},{9... | collective-permute-start | bytes 393224 | tf_op jit(solution)/shard_map/ppermute | solution.py:141
  79.6 0.7 copy-start.5
Sparse Core Ops, SparseCore 0:
  24.4 61.0 all-gather.3
  87.8 42.4 all-gather.5

commit v2 on v1

--- a/solution.py
+++ b/solution.py
@@ -4,6 +4,7 @@
 import jax.numpy as jnp
 from jax import lax
 from jax.sharding import PartitionSpec as P
+
 
 F32 = jnp.float32
 BF16 = jnp.bfloat16
@@ -104,11 +105,20 @@
     tap_count = short_taps.shape[0]
     sub = value_pre.shape[1] // n_seq
 
-    inputs_all = lax.all_gather(layer_input, "seq", axis=0, tiled=True)
+    half_cols = layer_input.shape[1] // 2
+    width = value_pre.shape[0]
+    inputs_sc = lax.all_gather(layer_input[:, :half_cols], "seq", axis=0, tiled=True)
+    input_slabs = layer_input[:, half_cols:].reshape(width, half_cols // width, width)
+    input_slabs = jnp.swapaxes(input_slabs, 0, 1).reshape(-1, sub, width)
+    input_slabs = jnp.broadcast_to(input_slabs[:, None], (input_slabs.shape[0], n_seq, sub, width))
 
     filt_high, filt_low = split_words(long_filter)
     sent = to_tokens_in_lanes(jnp.stack([value_pre, gate_act, key_act, grad_out, filt_high, filt_low]), n_seq)
+    sent = jnp.concatenate([sent, input_slabs], axis=0)
     got = lax.all_to_all(sent, "seq", split_axis=1, concat_axis=1, tiled=True)
+    chunks = half_cols // width
+    inputs_a2a = got[6:].reshape(chunks, width // sub, n_seq, sub, width)
+    inputs_a2a = jnp.transpose(inputs_a2a, (2, 1, 3, 0, 4)).reshape(n_seq * width, half_cols)
     value_t = got[0].astype(F32)
     gate_t = got[1].astype(F32)
     key_t = got[2].astype(F32)
@@ -154,7 +164,6 @@
 
     tap_rows = jnp.stack([jnp.sum(grad_conv * value_shifted[j], axis=(0, 2)) for j in range(tap_count)])
     taps_high, taps_low = split_words(tap_rows)
-    width = value_t.shape[2]
     taps_slab = jnp.pad(jnp.concatenate([taps_high, taps_low], axis=0).T, ((0, 0), (0, width - 2 * tap_count)))
     taps_slab = jnp.broadcast_to(taps_slab[None], value_t.shape)
     gf_high, gf_low = split_words(grad_filter)
@@ -167,8 +176,11 @@
     grad_filter = join_words(outs[3], outs[4])
 
     blocks = value_t.shape[0]
-    inputs_3 = inputs_all.reshape(blocks, width, inputs_all.shape[1])
-    grad_proj = jnp.einsum("pmi,cpom->ico", inputs_3, value_cols, preferred_element_type=F32)
+    parts = []
+    for inputs_half in (inputs_sc, inputs_a2a):
+        inputs_3 = inputs_half.reshape(blocks, width, inputs_half.shape[1])
+        parts.append(jnp.einsum("pmi,cpom->ico", inputs_3, value_cols, preferred_element_type=F32))
+    grad_proj = jnp.concatenate(parts, axis=0)
     grad_proj = grad_proj.reshape(grad_proj.shape[0], -1)
     return (outs[0], outs[1], outs[2], grad_taps, grad_filter, grad_proj)
 
@@ -192,6 +204,4 @@
         P("seq", "chan"),
         P("chan", "seq"),
     )
-    return jax.shard_map(
-        on_device, mesh=mesh, in_specs=in_specs, out_specs=out_specs, check_vma=False
-    )
+    return jax.shard_map(on_device, mesh=mesh, in_specs=in_specs, out_specs=out_specs, check_vma=False)

time: 143 us -> 197 us (1.38)
  waiting for transfers between devices: 54.2 us -> 107 us
  blocking collectives: 19.7 us -> 0 us
  starting transfers between devices: 11.8 us -> 24.2 us
  local copies, waits for them, and re-layouts: 16.2 us -> 19.6 us
  matrix products: 22.8 us -> 25.1 us
    all_gather x1, waiting for transfers between devices: 0.01 us -> 44 us  [on_device(): lax.all_gather(layer_input[:, :half_cols], 'seq', axis=0, tiled=True)]
    all_to_all x1 -> x0, blocking collectives: 19.7 us -> none  [on_device(): outs = lax.all_to_all(outs, 'seq', split_axis=1, concat_axis=1, tiled=True)]
    all_to_all x1, waiting for transfers between devices: 12.3 us -> 26.8 us  [on_device(): got = lax.all_to_all(sent, 'seq', split_axis=1, concat_axis=1, tiled=True)]
    all_to_all x0 -> x1, starting transfers between devices: none -> 14.4 us  [on_device(): outs = lax.all_to_all(outs, 'seq', split_axis=1, concat_axis=1, tiled=True)]
    all_to_all x0 -> x1, waiting for transfers between devices: none -> 8.36 us  [on_device(): outs = lax.all_to_all(outs, 'seq', split_axis=1, concat_axis=1, tiled=True)]
    ppermute x1, waiting for transfers between devices: 15.5 us -> 7.73 us  [on_device(): value_swapped = lax.ppermute(grad_value, ('seq', 'chan'), swap)]
    all_gather x1, waiting for transfers between devices: 25.7 us -> 20.1 us  [on_device(): value_cols = lax.all_gather(value_swapped, 'chan', axis=0, tiled=False)]
    dot_general x1 -> x2, matrix products: 3.58 us -> 6.04 us  [on_device(): jnp.einsum('pmi,cpom->ico', inputs_3, value_cols, preferred_element_type=...]
  transfers between devices with their start and end apart: 4 -> 5, of which waited for: 3 -> 5; matrix products, arithmetic and copies ran while one was open for 19% -> 6% of each run, Pallas kernels for 0% -> 0%
where the time goes in v2:
time: 197 us; the launch traced here: 196 us
  waiting for transfers between devices  107 us (54%)
  matrix products  25.1 us (13%)
  starting transfers between devices  24.2 us (12%)
  local copies, waits for them, and re-layouts  19.6 us (10%)
  between operations  14.8 us (8%)
  other arithmetic  4.54 us (2%)
    all_gather x1, waiting for transfers between devices, on_device(): lax.all_gather(layer_input[:, :half_cols], 'seq', axis=0, tiled=True)  44 us
    all_to_all x1, waiting for transfers between devices, on_device(): got = lax.all_to_all(sent, 'seq', split_axis=1, concat_axis=1, tiled=True)  26.8 us
    all_gather x1, waiting for transfers between devices, on_device(): value_cols = lax.all_gather(value_swapped, 'chan', axis=0, tiled=False)  20.1 us
    all_to_all x1, starting transfers between devices, on_device(): outs = lax.all_to_all(outs, 'seq', split_axis=1, concat_axis=1, tiled=True)  14.4 us
    unnamed x52, local copies, waits for them, and re-layouts  12.9 us
    all_to_all x1, waiting for transfers between devices, on_device(): outs = lax.all_to_all(outs, 'seq', split_axis=1, concat_axis=1, tiled=True)  8.36 us
    ppermute x1, waiting for transfers between devices, on_device(): value_swapped = lax.ppermute(grad_value, ('seq', 'chan'), swap)  7.73 us
    all_to_all x1, starting transfers between devices, on_device(): got = lax.all_to_all(sent, 'seq', split_axis=1, concat_axis=1, tiled=True)  7.57 us
  transfers between devices with their start and end apart: 5, of which 5 were waited for; matrix products, arithmetic and copies ran while one was open for 6% of the time, Pallas kernels for 0%

profile of v2, /device:TPU:1, one launch (start us, length us, event | category | flops | bytes accessed | tf_op | source)
XLA Modules:
  0.0 195.7 jit_solution(13080022596734729389)
XLA Ops:
  7.2 1.1 copy.62
  8.3 1.0 copy.58
  9.4 1.0 copy.59
  10.4 1.0 copy.60
  11.4 1.0 copy.61
  12.6 0.6 fusion.73
  13.3 0.2 broadcast_in_dim.5
  13.5 1.7 pad_maximum_fusion
  15.2 7.6 %all-to-all-start = ((bf16[14,16,32,128]{3,2,0,1:T(8,128)(2,1)}), bf16[14,16,32,128]{3,2,0,1:T(8,128)(2,1)S(1)}, u32[]{:S(2)}, u32[]{:S(2)}) async-start(bf16[14,16,32,128]{3,2,0,1:T(8,128)(2,1)} %pad_maximum_fusion), calls=%async_computation | async-start | bytes 3670016 | tf_op jit(solution)/shard_map/all_to_all | solution.py:118
  23.0 26.8 %all-to-all-done = bf16[14,16,32,128]{3,2,0,1:T(8,128)(2,1)S(1)} async-done(((bf16[14,16,32,128]{3,2,0,1:T(8,128)(2,1)}), bf16[14,16,32,128]{3,2,0,1:T(8,128)(2,1)S(1)}, u32[]{:S(2)}, u32[]{:S(2)}) %all-to-all-start) | async-done | bytes 1835040 | tf_op jit(solution)/shard_map/all_to_all | solution.py:118
  49.9 0.1 pad_slice_fusion.5
  50.1 0.1 pad_slice_fusion.7
  50.2 0.1 slice.278
  50.4 0.1 slice.280
  50.5 0.2 fusion.48
  50.7 1.8 fusion.24
  52.6 0.4 multiply_subtract_fusion.1
  53.0 0.5 copy-done.5
  53.5 2.2 %fusion.22 = f32[32,2,32,256]{3,2,1,0:T(8,128)S(1)} fusion(f32[128,256,1,1]{1,0,3,2:T(8,128)S(1)} %copy-done.5, f32[32,2,32,128]{3,0,2,1:T(8,128)S(1)} %get-tuple-element.39), kind=kOutput, calls=%fused_computation.28 | convolution fusion | flops 805306368 | bytes 3276800 | tf_op jit(solution)/shard_map/kscm,mn->kscn/dot_general | solution.py:50
  55.7 2.2 %convolution_add_fusion.1 = f32[32,2,32,256]{3,2,1,0:T(8,128)S(1)} fusion(f32[32,2,32,256]{3,2,1,0:T(8,128)S(1)} %fusion.22, f32[128,256,1,1]{1,0,3,2:T(8,128)S(1)} %copy-done.13, f32[32,2,32,128]{3,0,2,1:T(8,128)S(1)} %get-tuple-element.38), kind=kOutput, calls=%fused_computation.10 | convolution fusion | flops 805830656 | bytes 5373952 | tf_op jit(solution)/shard_map/kscm,mn->kscn/dot_general | solution.py:50
  58.0 1.0 fusion.29
  59.0 1.0 fusion.8
  60.0 0.1 multiply_subtract_fusion.2
  60.2 0.5 copy-done.16
  60.7 1.7 multiply_reduce_fusion.2
  62.5 0.1 pad_slice_fusion.1
  62.6 0.1 pad_slice_fusion.3
  62.8 0.1 slice.295
  62.9 0.1 slice.297
  63.1 1.3 fusion.50
  64.4 0.1 multiply_subtract_fusion.5
  64.5 1.2 fusion.32
  65.7 1.2 fusion.9
  66.9 0.3 multiply_add_fusion.3
  67.4 0.7 copy-done.4
  68.1 2.2 %fusion.17 = f32[32,2,32,256]{3,0,2,1:T(8,128)S(1)} fusion(f32[128,256,1,1]{1,0,3,2:T(8,128)S(1)} %copy-done.4, f32[32,2,32,128]{3,2,1,0:T(8,128)S(1)} %pad_maximum_fusion.1), kind=kOutput, calls=%fused_computation.22 | convolution fusion | flops 805306368 | bytes 3276800 | tf_op jit(solution)/shard_map/kscn,nm->kscm/dot_general | solution.py:59
  70.4 2.2 %convolution_add_fusion = f32[32,2,32,256]{3,0,2,1:T(8,128)S(1)} fusion(f32[32,2,32,256]{3,0,2,1:T(8,128)S(1)} %fusion.17, f32[128,256,1,1]{1,0,3,2:T(8,128)S(1)} %copy-done.12, f32[32,2,32,128]{3,2,1,0:T(8,128)S(1)} %pad_maximum_fusion.2), kind=kOutput, calls=%fused_computation.9 | convolution fusion | flops 805830656 | bytes 5373952 | tf_op jit(solution)/shard_map/kscn,nm->kscm/dot_general | solution.py:59
  72.6 0.2 multiply_subtract_fusion
  72.8 0.5 copy-done.14
  73.3 1.1 fusion
  74.5 0.2 fusion.59
  74.7 0.5 bitcast_dynamic-update-slice_fusion
  75.2 1.9 collective-permute-start
  77.1 7.7 %collective-permute-done = bf16[16,32,128]{2,0,1:T(8,128)(2,1)S(1)} collective-permute-done((bf16[16,32,128]{2,0,1:T(8,128)(2,1)S(1)}, bf16[16,32,128]{2,0,1:T(8,128)(2,1)S(1)}, u32[]{:S(2)}, u32[]{:S(2)}) %collective-permute-start) | collective-permute-done | bytes 131104 | tf_op jit(solution)/shard_map/ppermute | solution.py:151
  84.8 0.7 copy-done.7
  85.8 1.1 copy.80
  86.9 14.4 %all-to-all-start.1 = ((bf16[6,16,32,128]{3,2,0,1:T(8,128)(2,1)}), bf16[6,16,32,128]{3,2,0,1:T(8,128)(2,1)S(1)}, u32[]{:S(2)}, u32[]{:S(2)}) async-start(bf16[6,16,32,128]{3,2,0,1:T(8,128)(2,1)} %copy.80), calls=%async_computation.1 | async-start | bytes 1572864 | tf_op jit(solution)/shard_map/all_to_all | solution.py:171
  101.3 0.3 all-gather.4.cloned.1.call-start
  101.6 0.5 all-gather.4.cloned.1.call-update
  102.1 1.1 copy.163
  103.2 1.5 reshape.191
  104.7 8.4 %all-to-all-done.1 = bf16[6,16,32,128]{3,2,0,1:T(8,128)(2,1)S(1)} async-done(((bf16[6,16,32,128]{3,2,0,1:T(8,128)(2,1)}), bf16[6,16,32,128]{3,2,0,1:T(8,128)(2,1)S(1)}, u32[]{:S(2)}, u32[]{:S(2)}) %all-to-all-start.1) | async-done | bytes 786464 | tf_op jit(solution)/shard_map/all_to_all | solution.py:171
  113.3 0.8 copy.86
  114.0 0.8 copy.87
  114.8 0.8 copy.88
  115.6 0.8 copy.89
  116.4 0.1 convert_add_fusion
  116.6 0.7 copy.103
  117.3 20.1 %all-gather.6.cloned.1.call-done = bf16[256,32,128]{2,0,1:T(8,128)(2,1)} async-done(((bf16[16,32,128]{2,0,1:T(8,128)(2,1)}), bf16[256,32,128]{2,0,1:T(8,128)(2,1)}) %all-gather.6.cloned.1.call-update) | async-done | bytes 2097168 | tf_op jit(solution)/shard_map/all_gather | solution.py:152
  137.3 2.9 %fusion.13 = f32[256,16,32]{0,2,1:T(8,128)S(1)} fusion(bf16[16,128,256,1]{2,1,0,3:T(8,128)(2,1)S(1)} %copy-done.1, bf16[16,16,32,128]{3,1,0,2:T(8,128)(2,1)} %bitcast.183), kind=kOutput, calls=%fused_computation.16 | convolution fusion | flops 536870912 | bytes 3670016 | tf_op jit(solution)/shard_map/pmi,cpom->ico/dot_general | solution.py:182
  140.3 44.0 %all-gather.4.cloned.1.call-done = bf16[2048,256]{1,0:T(8,128)(2,1)} async-done(((bf16[128,256]{1,0:T(8,128)(2,1)}), bf16[2048,256]{1,0:T(8,128)(2,1)}) %all-gather.4.cloned.1.call-update) | async-done | bytes 1048592 | tf_op jit(solution)/shard_map/all_gather | solution.py:110
  184.3 3.1 %fusion.10 = f32[256,16,32]{0,2,1:T(8,128)S(1)} fusion(bf16[16,128,256,1]{2,1,0,3:T(8,128)(2,1)} %bitcast.185, bf16[16,16,32,128]{3,1,0,2:T(8,128)(2,1)} %bitcast.184), kind=kOutput, calls=%fused_computation.15 | convolution fusion | flops 536870912 | bytes 3670016 | tf_op jit(solution)/shard_map/pmi,cpom->ico/dot_general | solution.py:182
  187.4 0.1 pad_maximum_fusion.3
  187.5 1.3 copy.90
  (70 shorter events, 1.5 us)
Async XLA Ops:
  7.2 15.7 %copy-start = (f32[3,512]{1,0:T(4,128)S(1)}, f32[3,512]{1,0:T(4,128)}, u32[]{:S(2)}) copy-start(f32[3,512]{1,0:T(4,128)} %param.17) | copy-start | bytes 18436
  7.2 5.4 %copy-start.6 = (bf16[128,512]{1,0:T(8,128)(2,1)S(1)}, bf16[128,512]{1,0:T(8,128)(2,1)}, u32[]{:S(2)}) copy-start(bf16[128,512]{1,0:T(8,128)(2,1)} %param.13) | copy-start | bytes 393220
  15.2 34.5 %all-to-all-start = ((bf16[14,16,32,128]{3,2,0,1:T(8,128)(2,1)}), bf16[14,16,32,128]{3,2,0,1:T(8,128)(2,1)S(1)}, u32[]{:S(2)}, u32[]{:S(2)}) async-start(bf16[14,16,32,128]{3,2,0,1:T(8,128)(2,1)} %pad_maximum_fusion), calls=%async_computation | async-start | bytes 3670016 | tf_op jit(solution)/shard_map/all_to_all | solution.py:118
  22.8 114.6 %all-gather.6.cloned.1.call-start = ((), (), s32[]{:S(2)}) async-start(), calls=%async_computation.3 | async-start | bytes 2228224 | tf_op jit(solution)/shard_map/all_gather | solution.py:152
  49.9 0.8 copy-start.17
  50.4 2.2 %copy-start.2 = (f32[32,128]{1,0:T(8,128)S(1)}, f32[32,128]{1,0:T(8,128)}, u32[]{:S(2)}) copy-start(f32[32,128]{1,0:T(8,128)} %constant.48) | copy-start | bytes 49156
  50.4 2.2 %copy-start.3 = (f32[32,128]{1,0:T(8,128)S(1)}, f32[32,128]{1,0:T(8,128)}, u32[]{:S(2)}) copy-start(f32[32,128]{1,0:T(8,128)} %constant.49) | copy-start | bytes 49156
  52.6 0.9 copy-start.5
  52.9 2.8 %copy-start.13 = (f32[128,256,1,1]{1,0,3,2:T(8,128)S(1)}, f32[128,256,1,1]{1,0,3,2:T(8,128)}, u32[]{:S(2)}) copy-start(f32[128,256,1,1]{1,0,3,2:T(8,128)} %constant.57) | copy-start | bytes 393220
  55.7 2.3 %copy-start.9 = (f32[128,256,1]{1,0,2:T(8,128)S(1)}, f32[128,256,1]{1,0,2:T(8,128)}, u32[]{:S(2)}) copy-start(f32[128,256,1]{1,0,2:T(8,128)} %constant.64) | copy-start | bytes 393220
  55.7 3.3 %copy-start.11 = (f32[128,256,1]{1,0,2:T(8,128)S(1)}, f32[128,256,1]{1,0,2:T(8,128)}, u32[]{:S(2)}) copy-start(f32[128,256,1]{1,0,2:T(8,128)} %constant.65) | copy-start | bytes 393220
  60.0 0.7 copy-start.16
  62.4 0.7 copy-start.15
  63.0 1.5 copy-start.8
  64.4 1.3 copy-start.10
  67.2 0.9 copy-start.4
  68.1 2.2 %copy-start.12 = (f32[128,256,1,1]{1,0,3,2:T(8,128)S(1)}, f32[128,256,1,1]{1,0,3,2:T(8,128)}, u32[]{:S(2)}) copy-start(f32[128,256,1,1]{1,0,3,2:T(8,128)} %constant.62) | copy-start | bytes 393220
  72.6 0.7 copy-start.14
  75.2 9.7 %collective-permute-start = (bf16[16,32,128]{2,0,1:T(8,128)(2,1)S(1)}, bf16[16,32,128]{2,0,1:T(8,128)(2,1)S(1)}, u32[]{:S(2)}, u32[]{:S(2)}) collective-permute-start(bf16[16,32,128]{2,0,1:T(8,128)(2,1)S(1)} %get-tuple-element.31), channel_id=1, source_target_pairs={{0,0},{1,16},{2,32},{3,48},{4,64},{5,80},{6,96},{7,112},{8,128},{9... | collective-permute-start | bytes 393224 | tf_op jit(solution)/shard_map/ppermute | solution.py:151
  84.8 0.7 copy-start.7
  86.9 26.2 %all-to-all-start.1 = ((bf16[6,16,32,128]{3,2,0,1:T(8,128)(2,1)}), bf16[6,16,32,128]{3,2,0,1:T(8,128)(2,1)S(1)}, u32[]{:S(2)}, u32[]{:S(2)}) async-start(bf16[6,16,32,128]{3,2,0,1:T(8,128)(2,1)} %copy.80), calls=%async_computation.1 | async-start | bytes 1572864 | tf_op jit(solution)/shard_map/all_to_all | solution.py:171
  101.3 83.0 %all-gather.4.cloned.1.call-start = ((), (), s32[]{:S(2)}) async-start(), calls=%async_computation.2 | async-start | bytes 1114112 | tf_op jit(solution)/shard_map/all_gather | solution.py:110
  113.2 24.1 %copy-start.1 = (bf16[16,128,256,1]{2,1,0,3:T(8,128)(2,1)S(1)}, bf16[16,128,256,1]{2,1,0,3:T(8,128)(2,1)}, u32[]{:S(2)}) copy-start(bf16[16,128,256,1]{2,1,0,3:T(8,128)(2,1)} %reshape.191) | copy-start | bytes 3145732
Sparse Core Ops, SparseCore 0:
  85.6 51.6 all-gather.5
  139.8 44.4 all-gather.3

commit v3 on v1

--- a/solution.py
+++ b/solution.py
@@ -5,9 +5,12 @@
 from jax import lax
 from jax.sharding import PartitionSpec as P
 
+
 F32 = jnp.float32
 BF16 = jnp.bfloat16
 PRECISE = lax.Precision.HIGHEST
+SEQ = ("y", "x")
+CHAN = ("z", "core")
 
 
 def angles(rows, cols, period):
@@ -98,17 +101,18 @@
 
 
 def on_device(layer_input, value_pre, gate_act, key_act, short_taps, long_filter, grad_out):
-    n_seq = lax.axis_size("seq")
-    n_chan = lax.axis_size("chan")
-    me = lax.axis_index("seq")
+    n_seq = lax.axis_size(SEQ)
+    n_chan = lax.axis_size(CHAN)
+    me = lax.axis_index(SEQ)
     tap_count = short_taps.shape[0]
     sub = value_pre.shape[1] // n_seq
 
-    inputs_all = lax.all_gather(layer_input, "seq", axis=0, tiled=True)
+    inputs_all = lax.all_gather(layer_input, "x", axis=0, tiled=True)
+    inputs_all = lax.all_gather(inputs_all, "y", axis=0, tiled=True)
 
     filt_high, filt_low = split_words(long_filter)
     sent = to_tokens_in_lanes(jnp.stack([value_pre, gate_act, key_act, grad_out, filt_high, filt_low]), n_seq)
-    got = lax.all_to_all(sent, "seq", split_axis=1, concat_axis=1, tiled=True)
+    got = lax.all_to_all(sent, SEQ, split_axis=1, concat_axis=1, tiled=True)
     value_t = got[0].astype(F32)
     gate_t = got[1].astype(F32)
     key_t = got[2].astype(F32)
@@ -138,8 +142,10 @@
     grad_value = value_sum.astype(BF16)
 
     swap = [(a * n_chan + b, b * n_chan + a) for a in range(n_seq) for b in range(n_chan)]
-    value_swapped = lax.ppermute(grad_value, ("seq", "chan"), swap)
-    value_cols = lax.all_gather(value_swapped, "chan", axis=0, tiled=False)
+    value_swapped = lax.ppermute(grad_value, SEQ + CHAN, swap)
+    value_cols = lax.all_gather(value_swapped, "core", axis=0, tiled=False)
+    value_cols = lax.all_gather(value_cols, "z", axis=0, tiled=False)
+    value_cols = value_cols.reshape((-1,) + value_swapped.shape)
 
     sig_re, sig_im = spectra(signal[:, None], tables)
     prod_re = jnp.concatenate(
@@ -159,7 +165,7 @@
     taps_slab = jnp.broadcast_to(taps_slab[None], value_t.shape)
     gf_high, gf_low = split_words(grad_filter)
     outs = jnp.stack([grad_gate, grad_key, grad_value, gf_high, gf_low, taps_slab])
-    outs = lax.all_to_all(outs, "seq", split_axis=1, concat_axis=1, tiled=True)
+    outs = lax.all_to_all(outs, SEQ, split_axis=1, concat_axis=1, tiled=True)
     taps_got = outs[5, :, :, : 2 * tap_count]
     grad_taps = join_words(taps_got[..., :tap_count], taps_got[..., tap_count:])
     grad_taps = jnp.transpose(grad_taps, (2, 0, 1)).reshape(tap_count, -1)
@@ -174,24 +180,11 @@
 
 
 def solution(mesh):
-    assert mesh.shape["seq"] == mesh.shape["chan"]
-    in_specs = (
-        P("seq", "chan"),
-        P("seq", "chan"),
-        P("seq", "chan"),
-        P("seq", "chan"),
-        P(None, "chan"),
-        P("seq", "chan"),
-        P("seq", "chan"),
-    )
-    out_specs = (
-        P("seq", "chan"),
-        P("seq", "chan"),
-        P("seq", "chan"),
-        P(None, "chan"),
-        P("seq", "chan"),
-        P("chan", "seq"),
-    )
-    return jax.shard_map(
-        on_device, mesh=mesh, in_specs=in_specs, out_specs=out_specs, check_vma=False
-    )
+    seq_size, chan_size = mesh.shape["seq"], mesh.shape["chan"]
+    assert seq_size == chan_size and seq_size % 4 == 0 and chan_size % 2 == 0
+    grid = mesh.devices.reshape(4, seq_size // 4, chan_size // 2, 2)
+    fine = jax.sharding.Mesh(grid, ("y", "x", "z", "core"))
+    rows = P(SEQ, CHAN)
+    in_specs = (rows, rows, rows, rows, P(None, CHAN), rows, rows)
+    out_specs = (rows, rows, rows, P(None, CHAN), rows, P(CHAN, SEQ))
+    return jax.shard_map(on_device, mesh=fine, in_specs=in_specs, out_specs=out_specs, check_vma=False)

time: 143 us -> 143 us (level)
  the two profiles are of different devices: /device:TPU:1 before, /device:TPU:6 now
where the time goes in v3:
time: 143 us
  blocking collectives  45.2 us (32%)
  waiting for transfers between devices  30.8 us (22%)
  matrix products  22.7 us (16%)
  local copies, waits for them, and re-layouts  16.4 us (11%)
  between operations  14.7 us (10%)
  starting transfers between devices  10.2 us (7%)
  other arithmetic  2.64 us (2%)
    all_to_all x1, blocking collectives, on_device(): outs = lax.all_to_all(outs, SEQ, split_axis=1, concat_axis=1, tiled=True)  24.9 us
    all_gather x1, blocking collectives, on_device(): inputs_all = lax.all_gather(layer_input, 'x', axis=0, tiled=True)  18.4 us
    all_gather x1, waiting for transfers between devices, on_device(): value_cols = lax.all_gather(value_cols, 'z', axis=0, tiled=False)  18.2 us
    ppermute x1, waiting for transfers between devices, on_device(): value_swapped = lax.ppermute(grad_value, SEQ + CHAN, swap)  12.6 us
    unnamed x48, local copies, waits for them, and re-layouts  12.3 us
    all_to_all x1, starting transfers between devices, on_device(): got = lax.all_to_all(sent, SEQ, split_axis=1, concat_axis=1, tiled=True)  7.42 us
    dot_general x2, matrix products, spectra(): jnp.einsum('kscm,mn->kscn', turned_im, stage_b[width:], precision=PRECISE)  3.47 us
    dot_general x1, matrix products, on_device(): jnp.einsum('pmi,cpom->ico', inputs_3, value_cols, preferred_element_type=...  3.46 us
  transfers between devices with their start and end apart: 4, of which 2 were waited for; matrix products, arithmetic and copies ran while one was open for 20% of the time, Pallas kernels for 0%

profile of v3, /device:TPU:6, one launch (start us, length us, event | category | flops | bytes accessed | tf_op | source)
XLA Modules:
  0.0 142.6 jit_solution(12428216602779689207)
XLA Ops:
  7.2 1.0 copy.52
  8.2 1.0 copy.53
  9.3 1.0 copy.54
  10.3 1.0 copy.55
  11.3 1.1 copy.56
  12.6 1.0 copy.58
  13.5 7.4 %all-to-all-start = ((bf16[6,16,32,128]{3,2,0,1:T(8,128)(2,1)}), bf16[6,16,32,128]{3,2,0,1:T(8,128)(2,1)S(1)}, u32[]{:S(2)}, u32[]{:S(2)}) async-start(bf16[6,16,32,128]{3,2,0,1:T(8,128)(2,1)} %copy.58), calls=%async_computation | async-start | bytes 1572864 | tf_op jit(solution)/shard_map/all_to_all | solution.py:115
  21.0 18.4 %all_gather.22 = bf16[512,512]{1,0:T(8,128)(2,1)} all-gather(bf16[128,512]{1,0:T(8,128)(2,1)S(1)} %copy-done.3), channel_id=1, replica_groups=mesh['y'=4,'x'=4,'z'=8,'core'=2] {'x'}, dimensions={0}, use_global_device_ids=true | all-gather | bytes 655360 | tf_op jit(solution)/shard_map/all_gather | solution.py:110
  39.5 0.1 constant_dynamic-slice_fusion
  39.6 0.1 fusion.62
  39.8 0.1 pad_slice_fusion.7
  40.0 0.1 slice.266
  40.1 0.1 slice.268
  40.3 0.1 pad_slice_fusion.5
  40.5 0.2 fusion.38
  40.6 1.8 %fusion.14 = f32[64,2,32,128]{3,0,2,1:T(8,128)S(1)} fusion(f32[64,16,1,1]{0,1,3,2:T(8,128)S(1)} %copy-done.15, f32[16,1,32,128]{3,0,2,1:T(8,128)S(1)} %get-tuple-element.61, f32[16,1,32,128]{3,0,2,1:T(8,128)S(1)} %get-tuple-element.62), kind=kOutput, calls=%fused_computation.25 | convolution fusion | flops 100794368 | bytes 2625536 | tf_op jit(solution)/shard_map/kp,pscm->kscm/dot_general | solution.py:48
  42.5 0.3 multiply_subtract_fusion.1
  42.8 0.6 copy-done.5
  43.4 2.3 %fusion.12 = f32[32,2,32,256]{3,2,1,0:T(8,128)S(1)} fusion(f32[128,256,1,1]{1,0,3,2:T(8,128)S(1)} %copy-done.5, f32[32,2,32,128]{3,0,2,1:T(8,128)S(1)} %get-tuple-element.39), kind=kOutput, calls=%fused_computation.19 | convolution fusion | flops 805306368 | bytes 3276800 | tf_op jit(solution)/shard_map/kscm,mn->kscn/dot_general | solution.py:52
  45.7 2.3 %convolution_add_fusion.1 = f32[32,2,32,256]{3,2,1,0:T(8,128)S(1)} fusion(f32[32,2,32,256]{3,2,1,0:T(8,128)S(1)} %fusion.12, f32[128,256,1,1]{1,0,3,2:T(8,128)S(1)} %copy-done.11, f32[32,2,32,128]{3,0,2,1:T(8,128)S(1)} %get-tuple-element.38), kind=kOutput, calls=%fused_computation.5 | convolution fusion | flops 805830656 | bytes 5373952 | tf_op jit(solution)/shard_map/kscm,mn->kscn/dot_general | solution.py:52
  48.1 1.0 fusion.19
  49.0 1.0 fusion.4
  50.0 0.2 multiply_subtract_fusion.2
  50.2 0.1 maximum_bitcast_fusion
  50.3 0.4 copy-done.14
  50.7 1.7 %multiply_reduce_fusion.2 = (f32[32]{0:T(128)S(1)}, f32[32]{0:T(128)S(1)}, f32[32]{0:T(128)S(1)}, f32[16,32,128]{2,0,1:T(8,128)S(1)}, f32[16,32,128]{2,0,1:T(8,1...) fusion(bf16[1,16,32,128]{3,2,0,1:T(8,128)(2,1)S(1)} %get-tuple-element.44, ...), kind=kOutput, calls=%fused_computation.86 | convolution fusion | flops 51314592 | bytes 3412608 | tf_op jit(solution)/shard_map/pk,kscm->pscm/dot_general | solution.py:68
  52.5 0.1 slice.285
  52.6 0.1 pad_slice_fusion.1
  52.8 0.1 slice.283
  52.9 0.1 pad_slice_fusion.3
  53.1 0.1 copy-done.13
  53.1 1.3 fusion.40
  54.4 0.1 multiply_subtract_fusion.5
  54.6 1.2 fusion.22
  55.8 1.2 fusion.5
  56.9 0.3 multiply_add_fusion.3
  57.3 0.1 pad_maximum_fusion
  57.4 0.1 pad_maximum_fusion.1
  57.4 0.7 copy-done.4
  58.2 2.2 %fusion.7 = f32[32,2,32,256]{3,0,2,1:T(8,128)S(1)} fusion(f32[128,256,1,1]{1,0,3,2:T(8,128)S(1)} %copy-done.4, f32[32,2,32,128]{3,2,1,0:T(8,128)S(1)} %pad_maximum_fusion), kind=kOutput, calls=%fused_computation.14 | convolution fusion | flops 805306368 | bytes 3276800 | tf_op jit(solution)/shard_map/kscn,nm->kscm/dot_general | solution.py:61
  60.4 2.3 %convolution_add_fusion = f32[32,2,32,256]{3,0,2,1:T(8,128)S(1)} fusion(f32[32,2,32,256]{3,0,2,1:T(8,128)S(1)} %fusion.7, f32[128,256,1,1]{1,0,3,2:T(8,128)S(1)} %copy-done.10, f32[32,2,32,128]{3,2,1,0:T(8,128)S(1)} %pad_maximum_fusion.1), kind=kOutput, calls=%fused_computation.4 | convolution fusion | flops 805830656 | bytes 5373952 | tf_op jit(solution)/shard_map/kscn,nm->kscm/dot_general | solution.py:61
  62.7 0.2 multiply_subtract_fusion
  62.9 0.5 copy-done.12
  63.4 1.1 fusion
  64.5 0.1 fusion.53
  64.6 0.2 fusion.49
  64.8 0.5 bitcast_dynamic-update-slice_fusion
  65.3 2.7 %collective-permute-start = (bf16[16,32,128]{2,0,1:T(8,128)(2,1)S(1)}, bf16[16,32,128]{2,0,1:T(8,128)(2,1)S(1)}, u32[]{:S(2)}, u32[]{:S(2)}) collective-permute-start(bf16[16,32,128]{2,0,1:T(8,128)(2,1)S(1)} %get-tuple-element.31), channel_id=1, source_target_pairs={{0,0},{1,16},{2,32},{3,48},{4,64},{5,80},{6,96},{7,112},{8,128},{9... | collective-permute-start | bytes 393224 | tf_op jit(solution)/shard_map/ppermute | solution.py:145
  68.0 12.6 %collective-permute-done = bf16[16,32,128]{2,0,1:T(8,128)(2,1)S(1)} collective-permute-done((bf16[16,32,128]{2,0,1:T(8,128)(2,1)S(1)}, bf16[16,32,128]{2,0,1:T(8,128)(2,1)S(1)}, u32[]{:S(2)}, u32[]{:S(2)}) %collective-permute-start) | collective-permute-done | bytes 131104 | tf_op jit(solution)/shard_map/ppermute | solution.py:145
  80.5 2.0 %all-gather = bf16[32,32,128]{2,0,1:T(8,128)(2,1)S(1)} all-gather(bf16[16,32,128]{2,0,1:T(8,128)(2,1)S(1)} %collective-permute-done), channel_id=2, replica_groups=mesh['y'=4,'x'=4,'z'=8,'core'=2] {'core'}, dimensions={0}, use_global_device_ids=true | all-gather | bytes 393216 | tf_op jit(solution)/shard_map/all_gather | solution.py:146
  82.5 0.8 copy.76
  83.4 0.1 copy.101
  83.6 0.2 copy.73
  83.8 24.9 %all_to_all.10 = bf16[6,16,32,128]{3,2,0,1:T(8,128)(2,1)S(1)} all-to-all(bf16[6,16,32,128]{3,2,0,1:T(8,128)(2,1)S(1)} %copy.73), channel_id=1, replica_groups=mesh['y'=4,'x'=4,'z'=8,'core'=2] {'y','x'}, dimensions={1} | all-to-all | bytes 1572864 | tf_op jit(solution)/shard_map/all_to_all | solution.py:168
  108.7 0.1 copy.100
  108.8 0.8 copy.77
  109.6 0.8 copy.78
  110.4 0.8 copy.79
  111.2 0.1 convert_add_fusion
  111.3 0.7 copy.93
  112.0 0.8 copy.80
  112.9 18.2 %all-gather.7.cloned.1.call-done = bf16[16,16,32,128]{3,2,1,0:T(8,128)(2,1)} async-done(((bf16[2,16,32,128]{3,2,1,0:T(8,128)(2,1)}), bf16[16,16,32,128]{3,2,1,0:T(8,128)(2,1)}) %all-gather.7.cloned.1.call-update) | async-done | bytes 2097168 | tf_op jit(solution)/shard_map/all_gather | solution.py:147
  131.0 3.5 %fusion.63 = f32[16,32,512,1]{2,1,3,0:T(8,128)S(1)} fusion(bf16[16,16,32,128]{3,2,1,0:T(8,128)(2,1)} %all-gather.7.cloned.1.call-done, bf16[16,128,512,1]{2,1,0,3:T(8,128)(2,1)} %bitcast.171), kind=kOutput, calls=%fused_computation.136 | convolution fusion | flops 1073741824 | bytes 5242880 | tf_op jit(solution)/shard_map/pmi,cpom->ico/dot_general | solution.py:177
  134.5 1.3 copy.81
  (59 shorter events, 0.8 us)
Async XLA Ops:
  7.2 32.4 %copy-start = (f32[3,512]{1,0:T(4,128)S(1)}, f32[3,512]{1,0:T(4,128)}, u32[]{:S(2)}) copy-start(f32[3,512]{1,0:T(4,128)} %param.17) | copy-start | bytes 18436
  12.5 8.6 %copy-start.3 = (bf16[128,512]{1,0:T(8,128)(2,1)S(1)}, bf16[128,512]{1,0:T(8,128)(2,1)}, u32[]{:S(2)}) copy-start(bf16[128,512]{1,0:T(8,128)(2,1)} %param.13) | copy-start | bytes 393220
  13.5 26.1 %all-to-all-start = ((bf16[6,16,32,128]{3,2,0,1:T(8,128)(2,1)}), bf16[6,16,32,128]{3,2,0,1:T(8,128)(2,1)S(1)}, u32[]{:S(2)}, u32[]{:S(2)}) async-start(bf16[6,16,32,128]{3,2,0,1:T(8,128)(2,1)} %copy.58), calls=%async_computation | async-start | bytes 1572864 | tf_op jit(solution)/shard_map/all_to_all | solution.py:115
  21.0 91.9 %all-gather.5.cloned.1.call-start = ((), (), s32[]{:S(2)}) async-start(), calls=%async_computation.2 | async-start | bytes 2621440 | tf_op jit(solution)/shard_map/all_gather | solution.py:111
  39.5 91.6 %all-gather.7.cloned.1.call-start = ((), (), s32[]{:S(2)}) async-start(), calls=%async_computation.3 | async-start | bytes 2359296 | tf_op jit(solution)/shard_map/all_gather | solution.py:147
  39.8 0.8 copy-start.15
  40.3 2.2 %copy-start.1 = (f32[32,128]{1,0:T(8,128)S(1)}, f32[32,128]{1,0:T(8,128)}, u32[]{:S(2)}) copy-start(f32[32,128]{1,0:T(8,128)} %constant.56) | copy-start | bytes 49156
  40.3 2.2 %copy-start.2 = (f32[32,128]{1,0:T(8,128)S(1)}, f32[32,128]{1,0:T(8,128)}, u32[]{:S(2)}) copy-start(f32[32,128]{1,0:T(8,128)} %constant.55) | copy-start | bytes 49156
  42.5 0.9 copy-start.5
  42.8 2.9 %copy-start.11 = (f32[128,256,1,1]{1,0,3,2:T(8,128)S(1)}, f32[128,256,1,1]{1,0,3,2:T(8,128)}, u32[]{:S(2)}) copy-start(f32[128,256,1,1]{1,0,3,2:T(8,128)} %constant.64) | copy-start | bytes 393220
  45.7 2.3 %copy-start.7 = (f32[128,256,1]{1,0,2:T(8,128)S(1)}, f32[128,256,1]{1,0,2:T(8,128)}, u32[]{:S(2)}) copy-start(f32[128,256,1]{1,0,2:T(8,128)} %constant.71) | copy-start | bytes 393220
  45.7 3.3 %copy-start.9 = (f32[128,256,1]{1,0,2:T(8,128)S(1)}, f32[128,256,1]{1,0,2:T(8,128)}, u32[]{:S(2)}) copy-start(f32[128,256,1]{1,0,2:T(8,128)} %constant.72) | copy-start | bytes 393220
  50.0 0.7 copy-start.14
  52.4 0.7 copy-start.13
  53.1 1.5 %copy-start.6 = (f32[128,256,1]{1,0,2:T(8,128)S(1)}, f32[128,256,1]{1,0,2:T(8,128)}, u32[]{:S(2)}) copy-start(f32[128,256,1]{1,0,2:T(8,128)} %constant.66) | copy-start | bytes 393220
  54.4 1.3 copy-start.8
  57.3 0.9 copy-start.4
  58.2 2.2 %copy-start.10 = (f32[128,256,1,1]{1,0,3,2:T(8,128)S(1)}, f32[128,256,1,1]{1,0,3,2:T(8,128)}, u32[]{:S(2)}) copy-start(f32[128,256,1,1]{1,0,3,2:T(8,128)} %constant.69) | copy-start | bytes 393220
  62.7 0.7 copy-start.12
  65.3 15.3 %collective-permute-start = (bf16[16,32,128]{2,0,1:T(8,128)(2,1)S(1)}, bf16[16,32,128]{2,0,1:T(8,128)(2,1)S(1)}, u32[]{:S(2)}, u32[]{:S(2)}) collective-permute-start(bf16[16,32,128]{2,0,1:T(8,128)(2,1)S(1)} %get-tuple-element.31), channel_id=1, source_target_pairs={{0,0},{1,16},{2,32},{3,48},{4,64},{5,80},{6,96},{7,112},{8,128},{9... | collective-permute-start | bytes 393224 | tf_op jit(solution)/shard_map/ppermute | solution.py:145
Sparse Core Ops, SparseCore 0:
  39.6 36.7 all-gather.4
  83.5 47.4 all-gather.6

commit v4 on v1

--- a/solution.py
+++ b/solution.py
@@ -4,6 +4,7 @@
 import jax.numpy as jnp
 from jax import lax
 from jax.sharding import PartitionSpec as P
+
 
 F32 = jnp.float32
 BF16 = jnp.bfloat16
@@ -137,6 +138,9 @@
         value_sum = value_sum + taps[tap_index] * shift_ahead(grad_conv, tap_index, lane)
     grad_value = value_sum.astype(BF16)
 
+    grad_value, signal, filt_re, filt_im, grad_re, grad_im = lax.optimization_barrier(
+        (grad_value, signal, filt_re, filt_im, grad_re, grad_im)
+    )
     swap = [(a * n_chan + b, b * n_chan + a) for a in range(n_seq) for b in range(n_chan)]
     value_swapped = lax.ppermute(grad_value, ("seq", "chan"), swap)
     value_cols = lax.all_gather(value_swapped, "chan", axis=0, tiled=False)
@@ -192,6 +196,4 @@
         P("seq", "chan"),
         P("chan", "seq"),
     )
-    return jax.shard_map(
-        on_device, mesh=mesh, in_specs=in_specs, out_specs=out_specs, check_vma=False
-    )
+    return jax.shard_map(on_device, mesh=mesh, in_specs=in_specs, out_specs=out_specs, check_vma=False)

time: 143 us -> 136 us (0.951)
  waiting for transfers between devices: 54.2 us -> 36.4 us
  blocking collectives: 19.7 us -> 27.6 us
    ppermute x1, waiting for transfers between devices: 15.5 us -> 0.01 us  [on_device(): value_swapped = lax.ppermute(grad_value, ('seq', 'chan'), swap)]
    all_to_all x1, blocking collectives: 19.7 us -> 27.6 us  [on_device(): outs = lax.all_to_all(outs, 'seq', split_axis=1, concat_axis=1, tiled=True)]
    all_gather x1, waiting for transfers between devices: 25.7 us -> 23.4 us  [on_device(): value_cols = lax.all_gather(value_swapped, 'chan', axis=0, tiled=False)]
    unnamed x48 -> x71, local copies, waits for them, and re-layouts: 12.9 us -> 13.1 us
  transfers between devices with their start and end apart: 4 -> 4, of which waited for: 3 -> 2; matrix products, arithmetic and copies ran while one was open for 19% -> 23% of each run, Pallas kernels for 0% -> 0%
where the time goes in v4:
time: 136 us; the launch traced here: 135 us
  waiting for transfers between devices  36.4 us (27%)
  blocking collectives  27.6 us (20%)
  matrix products  24.2 us (18%)
  local copies, waits for them, and re-layouts  16.7 us (12%)
  between operations  14.9 us (11%)
  starting transfers between devices  12 us (9%)
  other arithmetic  3.44 us (3%)
    all_to_all x1, blocking collectives, on_device(): outs = lax.all_to_all(outs, 'seq', split_axis=1, concat_axis=1, tiled=True)  27.6 us
    all_gather x1, waiting for transfers between devices, on_device(): value_cols = lax.all_gather(value_swapped, 'chan', axis=0, tiled=False)  23.4 us
    unnamed x71, local copies, waits for them, and re-layouts  13.1 us
    all_to_all x1, waiting for transfers between devices, on_device(): got = lax.all_to_all(sent, 'seq', split_axis=1, concat_axis=1, tiled=True)  12.3 us
    all_to_all x1, starting transfers between devices, on_device(): got = lax.all_to_all(sent, 'seq', split_axis=1, concat_axis=1, tiled=True)  7.57 us
    ppermute x1, starting transfers between devices, on_device(): value_swapped = lax.ppermute(grad_value, ('seq', 'chan'), swap)  4.31 us
    dot_general x2, matrix products, signals_back(): jnp.einsum('kscn,nm->kscm', prod_im, back_b[width:], precision=PRECISE)  4.2 us
    dot_general x1, matrix products, on_device(): jnp.einsum('pmi,cpom->ico', inputs_3, value_cols, preferred_element_type=...  3.59 us
  transfers between devices with their start and end apart: 4, of which 2 were waited for; matrix products, arithmetic and copies ran while one was open for 23% of the time, Pallas kernels for 0%

profile of v4, /device:TPU:1, one launch (start us, length us, event | category | flops | bytes accessed | tf_op | source)
XLA Modules:
  0.0 135.2 jit_solution(9393081290640425200)
XLA Ops:
  7.2 1.0 copy.52
  8.2 1.0 copy.53
  9.3 1.0 copy.54
  10.3 1.0 copy.55
  11.3 1.1 copy.56
  12.6 1.0 copy.58
  13.5 7.6 %all-to-all-start = ((bf16[6,16,32,128]{3,2,0,1:T(8,128)(2,1)}), bf16[6,16,32,128]{3,2,0,1:T(8,128)(2,1)S(1)}, u32[]{:S(2)}, u32[]{:S(2)}) async-start(bf16[6,16,32,128]{3,2,0,1:T(8,128)(2,1)} %copy.58), calls=%async_computation | async-start | bytes 1572864 | tf_op jit(solution)/shard_map/all_to_all | solution.py:112
  21.2 0.7 all-gather.4.cloned.1.call-update
  21.9 0.1 constant_dynamic-slice_fusion
  22.0 12.3 %all-to-all-done = bf16[6,16,32,128]{3,2,0,1:T(8,128)(2,1)S(1)} async-done(((bf16[6,16,32,128]{3,2,0,1:T(8,128)(2,1)}), bf16[6,16,32,128]{3,2,0,1:T(8,128)(2,1)S(1)}, u32[]{:S(2)}, u32[]{:S(2)}) %all-to-all-start) | async-done | bytes 786464 | tf_op jit(solution)/shard_map/all_to_all | solution.py:112
  34.4 0.1 fusion.63
  34.4 0.1 copy_convert_fusion
  34.6 0.1 pad_slice_fusion.3
  34.7 0.1 slice.276
  34.8 0.1 slice.278
  35.0 0.2 fusion.32
  35.2 1.8 %fusion.16 = f32[64,2,32,128]{3,0,2,1:T(8,128)S(1)} fusion(f32[64,16,1,1]{0,1,3,2:T(8,128)S(1)} %copy-done.20, f32[16,1,32,128]{3,0,2,1:T(8,128)S(1)} %get-tuple-element.79, f32[16,1,32,128]{3,0,2,1:T(8,128)S(1)} %get-tuple-element.80), kind=kOutput, calls=%fused_computation.27 | convolution fusion | flops 100794368 | bytes 2625536 | tf_op jit(solution)/shard_map/kp,pscm->kscm/dot_general | solution.py:46
  37.1 0.4 multiply_subtract_fusion.1
  37.5 0.5 copy-done.11
  38.0 2.3 %fusion.14 = f32[32,2,32,256]{3,2,1,0:T(8,128)S(1)} fusion(f32[128,256,1,1]{1,0,3,2:T(8,128)S(1)} %copy-done.11, f32[32,2,32,128]{3,0,2,1:T(8,128)S(1)} %get-tuple-element.45), kind=kOutput, calls=%fused_computation.21 | convolution fusion | flops 805306368 | bytes 3276800 | tf_op jit(solution)/shard_map/kscm,mn->kscn/dot_general | solution.py:50
  40.3 2.3 %convolution_add_fusion.1 = f32[32,2,32,256]{3,2,1,0:T(8,128)S(1)} fusion(f32[32,2,32,256]{3,2,1,0:T(8,128)S(1)} %fusion.14, f32[128,256,1,1]{1,0,3,2:T(8,128)S(1)} %copy-done.16, f32[32,2,32,128]{3,0,2,1:T(8,128)S(1)} %get-tuple-element.44), kind=kOutput, calls=%fused_computation.7 | convolution fusion | flops 805830656 | bytes 5373952 | tf_op jit(solution)/shard_map/kscm,mn->kscn/dot_general | solution.py:50
  42.6 1.0 fusion.21
  43.6 1.0 fusion.7
  44.6 0.1 pad_slice_fusion.1
  44.8 0.1 multiply_subtract_fusion.5
  44.9 0.1 maximum_bitcast_fusion
  45.0 0.5 copy-done.19
  45.4 2.4 %multiply_reduce_fusion.2 = (f32[32]{0:T(128)S(1)}, f32[32]{0:T(128)S(1)}, f32[32]{0:T(128)S(1)}, f32[16,32,128]{2,0,1:T(8,128)S(1)}, f32[16,32,128]{2,0,1:T(8,1...) fusion(bf16[1,16,32,128]{3,2,0,1:T(8,128)(2,1)S(1)} %get-tuple-element.65, ...), kind=kOutput, calls=%fused_computation.79 | convolution fusion | flops 51314592 | bytes 3412608 | tf_op jit(solution)/shard_map/pk,kscm->pscm/dot_general | solution.py:66
  47.8 0.1 slice.272
  48.0 0.1 slice.270
  48.1 0.1 pad_slice_fusion.5
  48.3 0.1 pad_slice_fusion.7
  48.5 0.1 copy-done.1
  48.5 1.1 convert_multiply_fusion
  49.7 0.3 fusion.62
  50.0 0.1 copy.101
  50.1 4.3 %collective-permute-start = (bf16[16,32,128]{2,0,1:T(8,128)(2,1)}, bf16[16,32,128]{2,0,1:T(8,128)(2,1)}, u32[]{:S(2)}, u32[]{:S(2)}) collective-permute-start(bf16[16,32,128]{2,0,1:T(8,128)(2,1)} %get-tuple-element.17), channel_id=1, source_target_pairs={{0,0},{1,16},{2,32},{3,48},{4,64},{5,80},{6,96},{7,112},{8,128},{9... | collective-permute-start | bytes 393224 | tf_op jit(solution)/shard_map/ppermute | solution.py:145
  54.5 1.0 fusion.64
  55.5 0.2 multiply_subtract_fusion.4
  55.7 1.2 fusion.24
  56.8 1.2 fusion.6
  58.0 0.3 multiply_add_fusion.2
  58.4 0.1 pad_maximum_fusion
  58.4 0.8 copy-done.10
  59.3 2.2 %fusion.9 = f32[32,2,32,256]{3,0,2,1:T(8,128)S(1)} fusion(f32[128,256,1,1]{1,0,3,2:T(8,128)S(1)} %copy-done.10, f32[32,2,32,128]{3,2,1,0:T(8,128)S(1)} %pad_maximum_fusion), kind=kOutput, calls=%fused_computation.16 | convolution fusion | flops 805306368 | bytes 3276800 | tf_op jit(solution)/shard_map/kscn,nm->kscm/dot_general | solution.py:59
  61.5 0.1 pad_maximum_fusion.1
  61.6 3.2 %convolution_add_fusion = f32[32,2,32,256]{3,0,2,1:T(8,128)S(1)} fusion(f32[32,2,32,256]{3,0,2,1:T(8,128)S(1)} %fusion.9, f32[128,256,1,1]{1,0,3,2:T(8,128)} %constant.65, f32[32,2,32,128]{3,2,1,0:T(8,128)S(1)} %pad_maximum_fusion.1), kind=kOutput, calls=%fused_computation.6 | convolution fusion | flops 805830656 | bytes 5373952 | tf_op jit(solution)/shard_map/kscn,nm->kscm/dot_general | solution.py:59
  64.8 0.3 multiply_subtract_fusion
  65.2 0.3 copy-done.17
  65.5 1.1 fusion
  66.7 0.1 fusion.46
  66.8 0.2 fusion.42
  67.0 0.9 bitcast_dynamic-update-slice_fusion
  68.0 0.2 copy.73
  68.2 27.6 %all_to_all.10 = bf16[6,16,32,128]{3,2,0,1:T(8,128)(2,1)S(1)} all-to-all(bf16[6,16,32,128]{3,2,0,1:T(8,128)(2,1)S(1)} %copy.73), channel_id=1, replica_groups=mesh['seq'=16,'chan'=16] {'seq'}, dimensions={1} | all-to-all | bytes 1572864 | tf_op jit(solution)/shard_map/all_to_all | solution.py:166
  96.0 0.8 copy.77
  96.8 0.8 copy.78
  97.6 0.8 copy.79
  98.3 0.1 convert_add_fusion
  98.5 0.7 copy.93
  99.2 0.8 copy.80
  100.0 23.4 %all-gather.6.cloned.1.call-done = bf16[256,32,128]{2,0,1:T(8,128)(2,1)} async-done(((bf16[16,32,128]{2,0,1:T(8,128)(2,1)}), bf16[256,32,128]{2,0,1:T(8,128)(2,1)}) %all-gather.6.cloned.1.call-update) | async-done | bytes 2097168 | tf_op jit(solution)/shard_map/all_gather | solution.py:146
  123.4 3.6 %fusion.4 = f32[16,32,512,1]{2,1,3,0:T(8,128)S(1)} fusion(bf16[16,128,512,1]{2,1,0,3:T(8,128)(2,1)} %bitcast.168, bf16[16,16,32,128]{3,1,0,2:T(8,128)(2,1)} %bitcast.169), kind=kOutput, calls=%fused_computation.4 | convolution fusion | flops 1073741824 | bytes 5242880 | tf_op jit(solution)/shard_map/pmi,cpom->ico/dot_general | solution.py:175
  127.0 1.3 copy.81
  (80 shorter events, 0.9 us)
Async XLA Ops:
  7.2 14.8 %copy-start = (f32[3,512]{1,0:T(4,128)S(1)}, f32[3,512]{1,0:T(4,128)}, u32[]{:S(2)}) copy-start(f32[3,512]{1,0:T(4,128)} %param.17) | copy-start | bytes 18436
  13.5 20.8 %all-to-all-start = ((bf16[6,16,32,128]{3,2,0,1:T(8,128)(2,1)}), bf16[6,16,32,128]{3,2,0,1:T(8,128)(2,1)S(1)}, u32[]{:S(2)}, u32[]{:S(2)}) async-start(bf16[6,16,32,128]{3,2,0,1:T(8,128)(2,1)} %copy.58), calls=%async_computation | async-start | bytes 1572864 | tf_op jit(solution)/shard_map/all_to_all | solution.py:112
  21.1 78.9 %all-gather.4.cloned.1.call-start = ((), (), s32[]{:S(2)}) async-start(), calls=%async_computation.2 | async-start | bytes 2228224 | tf_op jit(solution)/shard_map/all_gather | solution.py:108
  21.9 101.5 %all-gather.6.cloned.1.call-start = ((), (), s32[]{:S(2)}) async-start(), calls=%async_computation.3 | async-start | bytes 2228224 | tf_op jit(solution)/shard_map/all_gather | solution.py:146
  22.0 26.4 %copy-start.21 = (f32[32]{0:T(128)}, f32[32]{0:T(128)S(1)}, u32[]{:S(2)}) copy-start(f32[32]{0:T(128)S(1)} %get-tuple-element.71) | copy-start | bytes 388
  22.0 26.4 %copy-start.23 = (f32[32]{0:T(128)}, f32[32]{0:T(128)S(1)}, u32[]{:S(2)}) copy-start(f32[32]{0:T(128)S(1)} %get-tuple-element.72) | copy-start | bytes 388
  22.0 26.4 %copy-start.25 = (f32[32]{0:T(128)}, f32[32]{0:T(128)S(1)}, u32[]{:S(2)}) copy-start(f32[32]{0:T(128)S(1)} %get-tuple-element.73) | copy-start | bytes 388
  34.4 0.8 copy-start.3
  34.5 0.7 copy-start.20
  35.0 2.1 %copy-start.6 = (f32[32,128]{1,0:T(8,128)S(1)}, f32[32,128]{1,0:T(8,128)}, u32[]{:S(2)}) copy-start(f32[32,128]{1,0:T(8,128)} %constant.49) | copy-start | bytes 49156
  35.0 2.1 %copy-start.8 = (f32[32,128]{1,0:T(8,128)S(1)}, f32[32,128]{1,0:T(8,128)}, u32[]{:S(2)}) copy-start(f32[32,128]{1,0:T(8,128)} %constant.48) | copy-start | bytes 49156
  37.1 0.9 copy-start.11
  37.5 2.8 %copy-start.16 = (f32[128,256,1,1]{1,0,3,2:T(8,128)S(1)}, f32[128,256,1,1]{1,0,3,2:T(8,128)}, u32[]{:S(2)}) copy-start(f32[128,256,1,1]{1,0,3,2:T(8,128)} %constant.58) | copy-start | bytes 393220
  40.3 2.3 %copy-start.13 = (f32[128,256,1]{1,0,2:T(8,128)S(1)}, f32[128,256,1]{1,0,2:T(8,128)}, u32[]{:S(2)}) copy-start(f32[128,256,1]{1,0,2:T(8,128)} %constant.59) | copy-start | bytes 393220
  40.3 3.3 %copy-start.15 = (f32[128,256,1]{1,0,2:T(8,128)S(1)}, f32[128,256,1]{1,0,2:T(8,128)}, u32[]{:S(2)}) copy-start(f32[128,256,1]{1,0,2:T(8,128)} %constant.60) | copy-start | bytes 393220
  44.7 0.7 copy-start.19
  47.8 0.7 copy-start.1
  49.7 4.8 %copy-start.18 = (f32[64,16,1]{0,1,2:T(8,128)S(1)}, f32[64,16,1]{0,1,2:T(8,128)}, u32[]{:S(2)}) copy-start(f32[64,16,1]{0,1,2:T(8,128)} %constant.61) | copy-start | bytes 12292
  50.0 5.7 %copy-start.12 = (f32[128,256,1]{1,0,2:T(8,128)S(1)}, f32[128,256,1]{1,0,2:T(8,128)}, u32[]{:S(2)}) copy-start(f32[128,256,1]{1,0,2:T(8,128)} %constant.62) | copy-start | bytes 393220
  50.1 11.4 %collective-permute-start = (bf16[16,32,128]{2,0,1:T(8,128)(2,1)}, bf16[16,32,128]{2,0,1:T(8,128)(2,1)}, u32[]{:S(2)}, u32[]{:S(2)}) collective-permute-start(bf16[16,32,128]{2,0,1:T(8,128)(2,1)} %get-tuple-element.17), channel_id=1, source_target_pairs={{0,0},{1,16},{2,32},{3,48},{4,64},{5,80},{6,96},{7,112},{8,128},{9... | collective-permute-start | bytes 393224 | tf_op jit(solution)/shard_map/ppermute | solution.py:145
  55.5 1.3 copy-start.14
  58.3 0.9 copy-start.10
  61.6 3.2 %copy-start.7 = (f32[32,128]{1,0:T(8,128)S(1)}, f32[32,128]{1,0:T(8,128)}, u32[]{:S(2)}) copy-start(f32[32,128]{1,0:T(8,128)} %constant.49) | copy-start | bytes 49156
  61.6 3.2 %copy-start.9 = (f32[32,128]{1,0:T(8,128)S(1)}, f32[32,128]{1,0:T(8,128)}, u32[]{:S(2)}) copy-start(f32[32,128]{1,0:T(8,128)} %constant.48) | copy-start | bytes 49156
  64.8 0.7 copy-start.17
  65.2 1.5 %copy-start.4 = (bf16[1,16,32,128]{3,2,0,1:T(8,128)(2,1)S(1)}, bf16[1,16,32,128]{3,2,0,1:T(8,128)(2,1)}, u32[]{:S(2)}) copy-start(bf16[1,16,32,128]{3,2,0,1:T(8,128)(2,1)} %copy-done.3) | copy-start | bytes 393220
  65.2 1.5 %copy-start.2 = (f32[16,32,128]{2,0,1:T(8,128)S(1)}, f32[16,32,128]{2,0,1:T(8,128)}, u32[]{:S(2)}) copy-start(f32[16,32,128]{2,0,1:T(8,128)} %copy-done.1) | copy-start | bytes 786436
  65.2 1.5 %copy-start.5 = (f32[16,32,128]{2,0,1:T(8,128)S(1)}, f32[16,32,128]{2,0,1:T(8,128)}, u32[]{:S(2)}) copy-start(f32[16,32,128]{2,0,1:T(8,128)} %get-tuple-element.78) | copy-start | bytes 786436
  65.2 1.5 %copy-start.22 = (f32[32]{0:T(128)S(1)}, f32[32]{0:T(128)}, u32[]{:S(2)}) copy-start(f32[32]{0:T(128)} %copy-done.21) | copy-start | bytes 388
  65.2 1.5 %copy-start.24 = (f32[32]{0:T(128)S(1)}, f32[32]{0:T(128)}, u32[]{:S(2)}) copy-start(f32[32]{0:T(128)} %copy-done.23) | copy-start | bytes 388
  65.2 1.5 %copy-start.26 = (f32[32]{0:T(128)S(1)}, f32[32]{0:T(128)}, u32[]{:S(2)}) copy-start(f32[32]{0:T(128)} %copy-done.25) | copy-start | bytes 388
Sparse Core Ops, SparseCore 0:
  24.4 56.6 all-gather.3
  82.8 40.5 all-gather.5

commit v5 on v4

--- a/solution.py
+++ b/solution.py
@@ -24,19 +24,23 @@
     twist = angles(freq_blocks, width, total)
     twist_cos = np.cos(twist)[:, None, None, :]
     twist_sin = np.sin(twist)[:, None, None, :]
-    inner = angles(width, width, width)
-    inner_cos, inner_sin = np.cos(inner), np.sin(inner)
-    stage_b = np.concatenate(
-        [np.concatenate([inner_cos, -inner_sin], axis=1), np.concatenate([inner_sin, inner_cos], axis=1)],
-        axis=0,
-    )
-    back_b = np.concatenate(
-        [np.concatenate([inner_cos, inner_sin], axis=1), np.concatenate([-inner_sin, inner_cos], axis=1)],
-        axis=0,
-    )
     back_a = np.concatenate([np.cos(outer).T, -np.sin(outer).T], axis=1) / total
     as_f32 = lambda a: jnp.asarray(a.astype(np.float32))
-    return tuple(as_f32(a) for a in (stage_a, twist_cos, twist_sin, stage_b, back_b, back_a))
+    rows = lax.broadcasted_iota(jnp.int32, (width, width), 0)
+    cols = lax.broadcasted_iota(jnp.int32, (width, width), 1)
+    product = lax.optimization_barrier(rows * cols % width)
+    inner = product.astype(F32) * (2.0 * np.pi / width)
+    inner_cos, inner_sin = jnp.cos(inner), jnp.sin(inner)
+    stage_b = jnp.concatenate(
+        [jnp.concatenate([inner_cos, -inner_sin], axis=1), jnp.concatenate([inner_sin, inner_cos], axis=1)],
+        axis=0,
+    )
+    back_b = jnp.concatenate(
+        [jnp.concatenate([inner_cos, inner_sin], axis=1), jnp.concatenate([-inner_sin, inner_cos], axis=1)],
+        axis=0,
+    )
+    stage_a, twist_cos, twist_sin, back_a = (as_f32(a) for a in (stage_a, twist_cos, twist_sin, back_a))
+    return stage_a, twist_cos, twist_sin, stage_b, back_b, back_a
 
 
 def spectra(stacked, tables):

time: 136 us -> 136 us (level)
    unnamed x71 -> x51, local copies, waits for them, and re-layouts: 13.1 us -> 11.7 us
where the time goes in v5:
time: 136 us
  waiting for transfers between devices  37.2 us (27%)
  blocking collectives  28.5 us (21%)
  matrix products  23.3 us (17%)
  local copies, waits for them, and re-layouts  16.3 us (12%)
  between operations  14.7 us (11%)
  starting transfers between devices  11.8 us (9%)
  other arithmetic  3.75 us (3%)
    all_to_all x1, blocking collectives, on_device(): outs = lax.all_to_all(outs, 'seq', split_axis=1, concat_axis=1, tiled=True)  28.5 us
    all_gather x1, waiting for transfers between devices, on_device(): value_cols = lax.all_gather(value_swapped, 'chan', axis=0, tiled=False)  24.4 us
    all_to_all x1, waiting for transfers between devices, on_device(): got = lax.all_to_all(sent, 'seq', split_axis=1, concat_axis=1, tiled=True)  12 us
    unnamed x51, local copies, waits for them, and re-layouts  11.7 us
    all_to_all x1, starting transfers between devices, on_device(): got = lax.all_to_all(sent, 'seq', split_axis=1, concat_axis=1, tiled=True)  7.57 us
    ppermute x1, starting transfers between devices, on_device(): value_swapped = lax.ppermute(grad_value, ('seq', 'chan'), swap)  4.13 us
    dot_general x1, matrix products, on_device(): jnp.einsum('pmi,cpom->ico', inputs_3, value_cols, preferred_element_type=...  3.58 us
    dot_general x2, matrix products, signals_back(): return jnp.einsum('pk,kscm->pscm', back_a, both, precision=PRECISE)  3.47 us
  transfers between devices with their start and end apart: 4, of which 2 were waited for; matrix products, arithmetic and copies ran while one was open for 23% of the time, Pallas kernels for 0%

profile of v5, /device:TPU:1, one launch (start us, length us, event | category | flops | bytes accessed | tf_op | source)
XLA Modules:
  0.0 135.5 jit_solution(9341757795906880837)
XLA Ops:
  7.2 1.0 copy.50
  8.2 1.0 copy.51
  9.3 1.0 copy.52
  10.3 1.0 copy.53
  11.3 1.1 copy.54
  12.5 0.1 fusion.45
  12.6 1.0 copy.56
  13.5 7.6 %all-to-all-start = ((bf16[6,16,32,128]{3,2,0,1:T(8,128)(2,1)}), bf16[6,16,32,128]{3,2,0,1:T(8,128)(2,1)S(1)}, u32[]{:S(2)}, u32[]{:S(2)}) async-start(bf16[6,16,32,128]{3,2,0,1:T(8,128)(2,1)} %copy.56), calls=%async_computation | async-start | bytes 1572864 | tf_op jit(solution)/shard_map/all_to_all | solution.py:116
  21.2 0.7 all-gather.4.cloned.1.call-update
  22.0 0.1 constant_dynamic-slice_fusion
  22.1 0.2 fusion.76
  22.3 12.0 %all-to-all-done = bf16[6,16,32,128]{3,2,0,1:T(8,128)(2,1)S(1)} async-done(((bf16[6,16,32,128]{3,2,0,1:T(8,128)(2,1)}), bf16[6,16,32,128]{3,2,0,1:T(8,128)(2,1)S(1)}, u32[]{:S(2)}, u32[]{:S(2)}) %all-to-all-start) | async-done | bytes 786464 | tf_op jit(solution)/shard_map/all_to_all | solution.py:116
  34.4 0.1 copy_convert_fusion
  34.6 0.1 pad_slice_fusion.3
  34.7 0.1 slice.256
  34.8 0.1 slice.258
  35.0 0.2 fusion.32
  35.2 1.8 %fusion.16 = f32[64,2,32,128]{3,0,2,1:T(8,128)S(1)} fusion(f32[64,16,1,1]{0,1,3,2:T(8,128)S(1)} %copy-done.16, f32[16,1,32,128]{3,0,2,1:T(8,128)S(1)} %get-tuple-element.82, f32[16,1,32,128]{3,0,2,1:T(8,128)S(1)} %get-tuple-element.83), kind=kOutput, calls=%fused_computation.27 | convolution fusion | flops 100794368 | bytes 2625536 | tf_op jit(solution)/shard_map/kp,pscm->kscm/dot_general | solution.py:50
  37.1 0.3 multiply_subtract_fusion.1
  37.4 2.3 %fusion.14 = f32[32,2,32,256]{3,2,1,0:T(8,128)S(1)} fusion(f32[32,2,32,128]{3,0,2,1:T(8,128)S(1)} %get-tuple-element.45, f32[128,128]{1,0:T(8,128)S(1)} %get-tuple-element.73, f32[128,128]{1,0:T(8,128)S(1)} %get-tuple-element.71), kind=kOutput, calls=%fused_computation.21 | convolution fusion | flops 805339136 | bytes 3276800 | tf_op jit(solution)/shard_map/kscm,mn->kscn/dot_general | solution.py:54
  39.7 2.3 %convolution_add_fusion.1 = f32[32,2,32,256]{3,2,1,0:T(8,128)S(1)} fusion(f32[32,2,32,256]{3,2,1,0:T(8,128)S(1)} %fusion.14, f32[32,2,32,128]{3,0,2,1:T(8,128)S(1)} %get-tuple-element.44, f32[128,128]{1,0:T(8,128)S(1)} %get-tuple-element.73, f32[128,128]{1,0:T(8,128)S(1)} %get-tuple-element.72), kind=kOutput, calls=%fused_computation.7 | convolution fusion | flops 805863424 | bytes 5373952 | tf_op jit(solution)/shard_map/kscm,mn->kscn/dot_general | solution.py:54
  42.0 1.0 fusion.21
  43.0 1.0 fusion.7
  44.0 0.1 pad_slice_fusion.1
  44.1 0.2 multiply_subtract_fusion.5
  44.3 0.1 maximum_bitcast_fusion
  44.4 0.4 copy-done.15
  44.8 2.4 %multiply_reduce_fusion.2 = (f32[32]{0:T(128)S(1)}, f32[32]{0:T(128)S(1)}, f32[32]{0:T(128)S(1)}, f32[16,32,128]{2,0,1:T(8,128)S(1)}, f32[16,32,128]{2,0,1:T(8,1...) fusion(bf16[1,16,32,128]{3,2,0,1:T(8,128)(2,1)S(1)} %get-tuple-element.65, ...), kind=kOutput, calls=%fused_computation.79 | convolution fusion | flops 51314592 | bytes 3412608 | tf_op jit(solution)/shard_map/pk,kscm->pscm/dot_general | solution.py:70
  47.2 0.1 slice.252
  47.3 0.1 slice.250
  47.5 0.1 pad_slice_fusion.5
  47.6 0.1 pad_slice_fusion.7
  47.8 0.1 copy-done.1
  47.9 1.2 convert_multiply_fusion
  49.0 1.3 fusion.85
  50.4 0.1 copy.99
  50.5 4.1 %collective-permute-start = (bf16[16,32,128]{2,0,1:T(8,128)(2,1)}, bf16[16,32,128]{2,0,1:T(8,128)(2,1)}, u32[]{:S(2)}, u32[]{:S(2)}) collective-permute-start(bf16[16,32,128]{2,0,1:T(8,128)(2,1)} %get-tuple-element.17), channel_id=1, source_target_pairs={{0,0},{1,16},{2,32},{3,48},{4,64},{5,80},{6,96},{7,112},{8,128},{9... | collective-permute-start | bytes 393224 | tf_op jit(solution)/shard_map/ppermute | solution.py:149
  54.7 1.0 fusion.87
  55.7 0.1 multiply_subtract_fusion.4
  55.9 1.2 fusion.24
  57.0 1.2 fusion.6
  58.2 0.4 multiply_add_fusion.2
  58.6 0.1 pad_maximum_fusion
  58.7 2.2 %fusion.9 = f32[32,2,32,256]{3,0,2,1:T(8,128)S(1)} fusion(f32[32,2,32,128]{3,2,1,0:T(8,128)S(1)} %pad_maximum_fusion, f32[128,128]{1,0:T(8,128)S(1)} %get-tuple-element.73, f32[128,128]{1,0:T(8,128)S(1)} %get-tuple-element.72), kind=kOutput, calls=%fused_computation.16 | convolution fusion | flops 805339136 | bytes 3276800 | tf_op jit(solution)/shard_map/kscn,nm->kscm/dot_general | solution.py:63
  60.9 0.1 pad_maximum_fusion.1
  61.0 2.3 %convolution_add_fusion = f32[32,2,32,256]{3,0,2,1:T(8,128)S(1)} fusion(f32[32,2,32,256]{3,0,2,1:T(8,128)S(1)} %fusion.9, f32[32,2,32,128]{3,2,1,0:T(8,128)S(1)} %pad_maximum_fusion.1, f32[128,128]{1,0:T(8,128)S(1)} %get-tuple-element.73, f32[128,128]{1,0:T(8,128)S(1)} %get-tuple-element.71), kind=kOutput, calls=%fused_computation.6 | convolution fusion | flops 805863424 | bytes 5373952 | tf_op jit(solution)/shard_map/kscn,nm->kscm/dot_general | solution.py:63
  63.3 0.3 multiply_subtract_fusion
  63.7 0.3 copy-done.13
  64.0 1.1 fusion
  65.1 0.1 fusion.46
  65.2 0.2 fusion.42
  65.4 0.9 bitcast_dynamic-update-slice_fusion
  66.5 0.2 copy.71
  66.7 28.5 %all_to_all.10 = bf16[6,16,32,128]{3,2,0,1:T(8,128)(2,1)S(1)} all-to-all(bf16[6,16,32,128]{3,2,0,1:T(8,128)(2,1)S(1)} %copy.71), channel_id=1, replica_groups=mesh['seq'=16,'chan'=16] {'seq'}, dimensions={1} | all-to-all | bytes 1572864 | tf_op jit(solution)/shard_map/all_to_all | solution.py:170
  95.3 0.1 copy.98
  95.4 0.8 copy.75
  96.1 0.8 copy.76
  96.9 0.8 copy.77
  97.7 0.1 convert_add_fusion
  97.8 0.7 copy.91
  98.5 0.8 copy.78
  99.4 24.4 %all-gather.6.cloned.1.call-done = bf16[256,32,128]{2,0,1:T(8,128)(2,1)} async-done(((bf16[16,32,128]{2,0,1:T(8,128)(2,1)}), bf16[256,32,128]{2,0,1:T(8,128)(2,1)}) %all-gather.6.cloned.1.call-update) | async-done | bytes 2097168 | tf_op jit(solution)/shard_map/all_gather | solution.py:150
  123.8 3.6 %fusion.4 = f32[16,32,512,1]{2,1,3,0:T(8,128)S(1)} fusion(bf16[16,128,512,1]{2,1,0,3:T(8,128)(2,1)} %bitcast.176, bf16[16,16,32,128]{3,1,0,2:T(8,128)(2,1)} %bitcast.177), kind=kOutput, calls=%fused_computation.4 | convolution fusion | flops 1073741824 | bytes 5242880 | tf_op jit(solution)/shard_map/pmi,cpom->ico/dot_general | solution.py:179
  127.4 1.3 copy.79
  (62 shorter events, 0.8 us)
Async XLA Ops:
  7.2 14.8 %copy-start = (f32[3,512]{1,0:T(4,128)S(1)}, f32[3,512]{1,0:T(4,128)}, u32[]{:S(2)}) copy-start(f32[3,512]{1,0:T(4,128)} %param.15) | copy-start | bytes 18436
  13.5 20.8 %all-to-all-start = ((bf16[6,16,32,128]{3,2,0,1:T(8,128)(2,1)}), bf16[6,16,32,128]{3,2,0,1:T(8,128)(2,1)S(1)}, u32[]{:S(2)}, u32[]{:S(2)}) async-start(bf16[6,16,32,128]{3,2,0,1:T(8,128)(2,1)} %copy.56), calls=%async_computation | async-start | bytes 1572864 | tf_op jit(solution)/shard_map/all_to_all | solution.py:116
  21.1 78.3 %all-gather.4.cloned.1.call-start = ((), (), s32[]{:S(2)}) async-start(), calls=%async_computation.2 | async-start | bytes 2228224 | tf_op jit(solution)/shard_map/all_gather | solution.py:112
  21.9 102.0 %all-gather.6.cloned.1.call-start = ((), (), s32[]{:S(2)}) async-start(), calls=%async_computation.3 | async-start | bytes 2228224 | tf_op jit(solution)/shard_map/all_gather | solution.py:150
  34.4 0.8 copy-start.8
  34.5 0.7 copy-start.16
  35.0 2.1 %copy-start.11 = (f32[32,128]{1,0:T(8,128)S(1)}, f32[32,128]{1,0:T(8,128)}, u32[]{:S(2)}) copy-start(f32[32,128]{1,0:T(8,128)} %constant.58) | copy-start | bytes 49156
  35.0 2.1 %copy-start.12 = (f32[32,128]{1,0:T(8,128)S(1)}, f32[32,128]{1,0:T(8,128)}, u32[]{:S(2)}) copy-start(f32[32,128]{1,0:T(8,128)} %constant.57) | copy-start | bytes 49156
  44.1 0.7 copy-start.15
  47.2 0.7 copy-start.1
  47.2 1.9 %copy-start.3 = (f32[16,32,128]{2,0,1:T(8,128)}, f32[16,32,128]{2,0,1:T(8,128)S(1)}, u32[]{:S(2)}) copy-start(f32[16,32,128]{2,0,1:T(8,128)S(1)} %get-tuple-element.40) | copy-start | bytes 786436
  49.0 5.6 %copy-start.14 = (f32[64,16,1]{0,1,2:T(8,128)S(1)}, f32[64,16,1]{0,1,2:T(8,128)}, u32[]{:S(2)}) copy-start(f32[64,16,1]{0,1,2:T(8,128)} %constant.62) | copy-start | bytes 12292
  50.5 10.5 %collective-permute-start = (bf16[16,32,128]{2,0,1:T(8,128)(2,1)}, bf16[16,32,128]{2,0,1:T(8,128)(2,1)}, u32[]{:S(2)}, u32[]{:S(2)}) collective-permute-start(bf16[16,32,128]{2,0,1:T(8,128)(2,1)} %get-tuple-element.17), channel_id=1, source_target_pairs={{0,0},{1,16},{2,32},{3,48},{4,64},{5,80},{6,96},{7,112},{8,128},{9... | collective-permute-start | bytes 393224 | tf_op jit(solution)/shard_map/ppermute | solution.py:149
  55.8 2.4 %copy-start.5 = (f32[32,1,32,128]{3,2,1,0:T(8,128)S(1)}, f32[32,1,32,128]{3,2,1,0:T(8,128)}, u32[]{:S(2)}) copy-start(f32[32,1,32,128]{3,2,1,0:T(8,128)} %get-tuple-element.14) | copy-start | bytes 1572868
  55.8 2.4 %copy-start.6 = (f32[32,1,32,128]{3,2,1,0:T(8,128)S(1)}, f32[32,1,32,128]{3,2,1,0:T(8,128)}, u32[]{:S(2)}) copy-start(f32[32,1,32,128]{3,2,1,0:T(8,128)} %get-tuple-element.15) | copy-start | bytes 1572868
  55.8 2.4 %copy-start.7 = (f32[32,1,32,128]{3,2,1,0:T(8,128)S(1)}, f32[32,1,32,128]{3,2,1,0:T(8,128)}, u32[]{:S(2)}) copy-start(f32[32,1,32,128]{3,2,1,0:T(8,128)} %get-tuple-element.12) | copy-start | bytes 1572868
  63.3 0.7 copy-start.13
  63.6 1.5 %copy-start.9 = (bf16[1,16,32,128]{3,2,0,1:T(8,128)(2,1)S(1)}, bf16[1,16,32,128]{3,2,0,1:T(8,128)(2,1)}, u32[]{:S(2)}) copy-start(bf16[1,16,32,128]{3,2,0,1:T(8,128)(2,1)} %copy-done.8) | copy-start | bytes 393220
  63.7 1.5 %copy-start.2 = (f32[16,32,128]{2,0,1:T(8,128)S(1)}, f32[16,32,128]{2,0,1:T(8,128)}, u32[]{:S(2)}) copy-start(f32[16,32,128]{2,0,1:T(8,128)} %copy-done.1) | copy-start | bytes 786436
  63.7 1.5 %copy-start.4 = (f32[16,32,128]{2,0,1:T(8,128)S(1)}, f32[16,32,128]{2,0,1:T(8,128)}, u32[]{:S(2)}) copy-start(f32[16,32,128]{2,0,1:T(8,128)} %copy-done.3) | copy-start | bytes 786436
  63.7 1.5 %copy-start.10 = (f32[16,32,128]{2,0,1:T(8,128)S(1)}, f32[16,32,128]{2,0,1:T(8,128)}, u32[]{:S(2)}) copy-start(f32[16,32,128]{2,0,1:T(8,128)} %get-tuple-element.81) | copy-start | bytes 786436
Sparse Core Ops, SparseCore 0:
  24.4 57.0 all-gather.3
  83.2 40.5 all-gather.5

commit v6 on v3

--- a/solution.py
+++ b/solution.py
@@ -10,6 +10,7 @@
 BF16 = jnp.bfloat16
 PRECISE = lax.Precision.HIGHEST
 SEQ = ("y", "x")
+SEQ_NAME, CHAN_NAME = "seq", "chan"
 CHAN = ("z", "core")
 
 
@@ -26,19 +27,23 @@
     twist = angles(freq_blocks, width, total)
     twist_cos = np.cos(twist)[:, None, None, :]
     twist_sin = np.sin(twist)[:, None, None, :]
-    inner = angles(width, width, width)
-    inner_cos, inner_sin = np.cos(inner), np.sin(inner)
-    stage_b = np.concatenate(
-        [np.concatenate([inner_cos, -inner_sin], axis=1), np.concatenate([inner_sin, inner_cos], axis=1)],
+    back_a = np.concatenate([np.cos(outer).T, -np.sin(outer).T], axis=1) / total
+    as_f32 = lambda a: jnp.asarray(a.astype(np.float32))
+    rows = lax.broadcasted_iota(jnp.int32, (width, width), 0)
+    cols = lax.broadcasted_iota(jnp.int32, (width, width), 1)
+    product = lax.optimization_barrier(rows * cols % width)
+    inner = product.astype(F32) * (2.0 * np.pi / width)
+    inner_cos, inner_sin = jnp.cos(inner), jnp.sin(inner)
+    stage_b = jnp.concatenate(
+        [jnp.concatenate([inner_cos, -inner_sin], axis=1), jnp.concatenate([inner_sin, inner_cos], axis=1)],
         axis=0,
     )
-    back_b = np.concatenate(
-        [np.concatenate([inner_cos, inner_sin], axis=1), np.concatenate([-inner_sin, inner_cos], axis=1)],
+    back_b = jnp.concatenate(
+        [jnp.concatenate([inner_cos, inner_sin], axis=1), jnp.concatenate([-inner_sin, inner_cos], axis=1)],
         axis=0,
     )
-    back_a = np.concatenate([np.cos(outer).T, -np.sin(outer).T], axis=1) / total
-    as_f32 = lambda a: jnp.asarray(a.astype(np.float32))
-    return tuple(as_f32(a) for a in (stage_a, twist_cos, twist_sin, stage_b, back_b, back_a))
+    stage_a, twist_cos, twist_sin, back_a = (as_f32(a) for a in (stage_a, twist_cos, twist_sin, back_a))
+    return stage_a, twist_cos, twist_sin, stage_b, back_b, back_a
 
 
 def spectra(stacked, tables):
@@ -141,11 +146,12 @@
         value_sum = value_sum + taps[tap_index] * shift_ahead(grad_conv, tap_index, lane)
     grad_value = value_sum.astype(BF16)
 
+    grad_value, signal, filt_re, filt_im, grad_re, grad_im = lax.optimization_barrier(
+        (grad_value, signal, filt_re, filt_im, grad_re, grad_im)
+    )
     swap = [(a * n_chan + b, b * n_chan + a) for a in range(n_seq) for b in range(n_chan)]
     value_swapped = lax.ppermute(grad_value, SEQ + CHAN, swap)
-    value_cols = lax.all_gather(value_swapped, "core", axis=0, tiled=False)
-    value_cols = lax.all_gather(value_cols, "z", axis=0, tiled=False)
-    value_cols = value_cols.reshape((-1,) + value_swapped.shape)
+    value_cols = lax.all_gather(value_swapped, CHAN, axis=0, tiled=False)
 
     sig_re, sig_im = spectra(signal[:, None], tables)
     prod_re = jnp.concatenate(
@@ -163,14 +169,13 @@
     width = value_t.shape[2]
     taps_slab = jnp.pad(jnp.concatenate([taps_high, taps_low], axis=0).T, ((0, 0), (0, width - 2 * tap_count)))
     taps_slab = jnp.broadcast_to(taps_slab[None], value_t.shape)
-    gf_high, gf_low = split_words(grad_filter)
-    outs = jnp.stack([grad_gate, grad_key, grad_value, gf_high, gf_low, taps_slab])
+    outs = jnp.stack([grad_gate, grad_key, grad_value, grad_filter.astype(BF16), taps_slab])
     outs = lax.all_to_all(outs, SEQ, split_axis=1, concat_axis=1, tiled=True)
-    taps_got = outs[5, :, :, : 2 * tap_count]
+    taps_got = outs[4, :, :, : 2 * tap_count]
     grad_taps = join_words(taps_got[..., :tap_count], taps_got[..., tap_count:])
     grad_taps = jnp.transpose(grad_taps, (2, 0, 1)).reshape(tap_count, -1)
-    outs = from_tokens_in_lanes(outs[:5])
-    grad_filter = join_words(outs[3], outs[4])
+    outs = from_tokens_in_lanes(outs[:4])
+    grad_filter = outs[3].astype(F32)
 
     blocks = value_t.shape[0]
     inputs_3 = inputs_all.reshape(blocks, width, inputs_all.shape[1])
@@ -180,10 +185,10 @@
 
 
 def solution(mesh):
-    seq_size, chan_size = mesh.shape["seq"], mesh.shape["chan"]
+    seq_size, chan_size = mesh.shape[SEQ_NAME], mesh.shape[CHAN_NAME]
     assert seq_size == chan_size and seq_size % 4 == 0 and chan_size % 2 == 0
     grid = mesh.devices.reshape(4, seq_size // 4, chan_size // 2, 2)
-    fine = jax.sharding.Mesh(grid, ("y", "x", "z", "core"))
+    fine = jax.sharding.Mesh(grid, SEQ + CHAN)
     rows = P(SEQ, CHAN)
     in_specs = (rows, rows, rows, rows, P(None, CHAN), rows, rows)
     out_specs = (rows, rows, rows, P(None, CHAN), rows, P(CHAN, SEQ))

time: 143 us -> 137 us (0.958)
  the two profiles are of different devices: /device:TPU:6 before, /device:TPU:1 now
where the time goes in v6:
time: 137 us; the launch traced here: 136 us
  blocking collectives  45.2 us (33%)
  waiting for transfers between devices  24.7 us (18%)
  matrix products  22.6 us (16%)
  between operations  14.7 us (11%)
  local copies, waits for them, and re-layouts  14.3 us (10%)
  starting transfers between devices  11.9 us (9%)
  other arithmetic  3.12 us (2%)
    all_to_all x1, blocking collectives, on_device(): outs = lax.all_to_all(outs, SEQ, split_axis=1, concat_axis=1, tiled=True)  26.6 us
    all_gather x1, waiting for transfers between devices, on_device(): value_cols = lax.all_gather(value_swapped, CHAN, axis=0, tiled=False)  24.7 us
    all_gather x1, blocking collectives, on_device(): inputs_all = lax.all_gather(layer_input, 'x', axis=0, tiled=True)  18.5 us
    unnamed x34, local copies, waits for them, and re-layouts  10.6 us
    all_to_all x1, starting transfers between devices, on_device(): got = lax.all_to_all(sent, SEQ, split_axis=1, concat_axis=1, tiled=True)  7.57 us
    ppermute x1, starting transfers between devices, on_device(): value_swapped = lax.ppermute(grad_value, SEQ + CHAN, swap)  4.26 us
    dot_general x1, matrix products, on_device(): jnp.einsum('pmi,cpom->ico', inputs_3, value_cols, preferred_element_type=...  3.58 us
    dot_general x2, matrix products, spectra(): jnp.einsum('kscm,mn->kscn', turned_im, stage_b[width:], precision=PRECISE)  3.46 us
  transfers between devices with their start and end apart: 4, of which 1 were waited for; matrix products, arithmetic and copies ran while one was open for 21% of the time, Pallas kernels for 0%

profile of v6, /device:TPU:1, one launch (start us, length us, event | category | flops | bytes accessed | tf_op | source)
XLA Modules:
  0.0 136.5 jit_solution(8983030592431116036)
XLA Ops:
  7.2 1.0 copy.50
  8.2 1.0 copy.51
  9.3 1.0 copy.52
  10.3 1.0 copy.53
  11.3 1.1 copy.54
  12.5 0.1 fusion.45
  12.6 1.0 copy.56
  13.5 7.6 %all-to-all-start = ((bf16[6,16,32,128]{3,2,0,1:T(8,128)(2,1)}), bf16[6,16,32,128]{3,2,0,1:T(8,128)(2,1)S(1)}, u32[]{:S(2)}, u32[]{:S(2)}) async-start(bf16[6,16,32,128]{3,2,0,1:T(8,128)(2,1)} %copy.56), calls=%async_computation | async-start | bytes 1572864 | tf_op jit(solution)/shard_map/all_to_all | solution.py:120
  21.1 0.0 all-gather.4.cloned.1.call-start
  21.2 18.5 %all_gather.14 = bf16[512,512]{1,0:T(8,128)(2,1)} all-gather(bf16[128,512]{1,0:T(8,128)(2,1)S(1)} %copy-done.3), channel_id=1, replica_groups=mesh['y'=4,'x'=4,'z'=8,'core'=2] {'x'}, dimensions={0}, use_global_device_ids=true | all-gather | bytes 655360 | tf_op jit(solution)/shard_map/all_gather | solution.py:115
  39.8 0.0 all-gather.6.cloned.1.call-start
  39.9 0.1 constant_dynamic-slice_fusion
  40.0 0.2 fusion.76
  40.2 0.1 fusion.86
  40.3 0.1 copy_convert_fusion
  40.5 0.1 pad_slice_fusion.3
  40.6 0.2 fusion.32
  40.8 0.1 copy-done.7
  40.9 1.8 %fusion.16 = f32[64,2,32,128]{3,0,2,1:T(8,128)S(1)} fusion(f32[64,16,1,1]{0,1,3,2:T(8,128)S(1)} %copy-done.7, f32[16,1,32,128]{3,0,2,1:T(8,128)S(1)} %get-tuple-element.83, f32[16,1,32,128]{3,0,2,1:T(8,128)S(1)} %get-tuple-element.84), kind=kOutput, calls=%fused_computation.27 | convolution fusion | flops 100794368 | bytes 2625536 | tf_op jit(solution)/shard_map/kp,pscm->kscm/dot_general | solution.py:53
  42.8 0.4 multiply_subtract_fusion.1
  43.2 2.3 %fusion.14 = f32[32,2,32,256]{3,2,1,0:T(8,128)S(1)} fusion(f32[32,2,32,128]{3,0,2,1:T(8,128)S(1)} %get-tuple-element.45, f32[128,128]{1,0:T(8,128)S(1)} %get-tuple-element.74, f32[128,128]{1,0:T(8,128)S(1)} %get-tuple-element.72), kind=kOutput, calls=%fused_computation.21 | convolution fusion | flops 805339136 | bytes 3276800 | tf_op jit(solution)/shard_map/kscm,mn->kscn/dot_general | solution.py:57
  45.4 2.3 %convolution_add_fusion.1 = f32[32,2,32,256]{3,2,1,0:T(8,128)S(1)} fusion(f32[32,2,32,256]{3,2,1,0:T(8,128)S(1)} %fusion.14, f32[32,2,32,128]{3,0,2,1:T(8,128)S(1)} %get-tuple-element.44, f32[128,128]{1,0:T(8,128)S(1)} %get-tuple-element.74, f32[128,128]{1,0:T(8,128)S(1)} %get-tuple-element.73), kind=kOutput, calls=%fused_computation.7 | convolution fusion | flops 805863424 | bytes 5373952 | tf_op jit(solution)/shard_map/kscm,mn->kscn/dot_general | solution.py:57
  47.8 1.0 fusion.21
  48.7 1.0 fusion.7
  49.7 0.2 multiply_subtract_fusion.5
  50.0 0.1 slice.253
  50.1 0.1 slice.255
  50.2 0.1 pad_slice_fusion.1
  50.4 0.1 maximum_bitcast_fusion
  50.4 0.2 copy-done.6
  50.6 1.8 %multiply_reduce_fusion.2 = (f32[32]{0:T(128)S(1)}, f32[32]{0:T(128)S(1)}, f32[32]{0:T(128)S(1)}, f32[16,32,128]{2,0,1:T(8,128)S(1)}, f32[16,32,128]{2,0,1:T(8,1...) fusion(bf16[1,16,32,128]{3,2,0,1:T(8,128)(2,1)S(1)} %get-tuple-element.65, ...), kind=kOutput, calls=%fused_computation.75 | convolution fusion | flops 51314592 | bytes 3412608 | tf_op jit(solution)/shard_map/pk,kscm->pscm/dot_general | solution.py:73
  52.4 0.1 slice.249
  52.6 0.1 slice.247
  52.7 0.1 pad_slice_fusion.5
  52.9 0.1 pad_slice_fusion.7
  53.0 0.5 convert_multiply_fusion
  53.5 0.4 fusion.85
  54.0 4.3 %collective-permute-start = (bf16[16,32,128]{2,0,1:T(8,128)(2,1)S(1)}, bf16[16,32,128]{2,0,1:T(8,128)(2,1)}, u32[]{:S(2)}, u32[]{:S(2)}) collective-permute-start(bf16[16,32,128]{2,0,1:T(8,128)(2,1)S(1)} %get-tuple-element.17), channel_id=1, source_target_pairs={{0,0},{1,16},{2,32},{3,48},{4,64},{5,80},{6,96},{7,112},{8,128},{9... | collective-permute-start | bytes 393224 | tf_op jit(solution)/shard_map/ppermute | solution.py:153
  58.3 1.0 fusion.87
  59.3 0.2 multiply_subtract_fusion.4
  59.4 1.2 fusion.24
  60.6 1.2 fusion.6
  61.8 0.4 multiply_add_fusion.2
  62.2 0.1 copy.99
  62.3 0.1 pad_maximum_fusion
  62.4 0.1 pad_maximum_fusion.1
  62.5 2.2 %fusion.9 = f32[32,2,32,256]{3,0,2,1:T(8,128)S(1)} fusion(f32[32,2,32,128]{3,2,1,0:T(8,128)S(1)} %pad_maximum_fusion, f32[128,128]{1,0:T(8,128)S(1)} %get-tuple-element.74, f32[128,128]{1,0:T(8,128)S(1)} %get-tuple-element.73), kind=kOutput, calls=%fused_computation.16 | convolution fusion | flops 805339136 | bytes 3276800 | tf_op jit(solution)/shard_map/kscn,nm->kscm/dot_general | solution.py:66
  64.7 2.2 %convolution_add_fusion = f32[32,2,32,256]{3,0,2,1:T(8,128)S(1)} fusion(f32[32,2,32,256]{3,0,2,1:T(8,128)S(1)} %fusion.9, f32[32,2,32,128]{3,2,1,0:T(8,128)S(1)} %pad_maximum_fusion.1, f32[128,128]{1,0:T(8,128)S(1)} %get-tuple-element.74, f32[128,128]{1,0:T(8,128)S(1)} %get-tuple-element.72), kind=kOutput, calls=%fused_computation.6 | convolution fusion | flops 805863424 | bytes 5373952 | tf_op jit(solution)/shard_map/kscn,nm->kscm/dot_general | solution.py:66
  67.0 0.3 multiply_subtract_fusion
  67.3 0.4 copy-done.4
  67.7 1.1 fusion
  68.8 0.1 fusion.46
  68.8 0.2 fusion.41
  69.1 0.2 copy.71
  69.3 26.6 %all_to_all.10 = bf16[5,16,32,128]{3,2,0,1:T(8,128)(2,1)S(1)} all-to-all(bf16[5,16,32,128]{3,2,0,1:T(8,128)(2,1)S(1)} %copy.71), channel_id=1, replica_groups=mesh['y'=4,'x'=4,'z'=8,'core'=2] {'y','x'}, dimensions={1} | all-to-all | bytes 1310720 | tf_op jit(solution)/shard_map/all_to_all | solution.py:173
  96.1 0.8 copy.75
  96.9 0.8 copy.76
  97.7 0.8 copy.77
  98.4 0.1 convert_add_fusion
  98.5 0.7 copy.91
  99.3 0.8 copy.78
  100.1 24.7 %all-gather.6.cloned.1.call-done = bf16[256,32,128]{2,0,1:T(8,128)(2,1)} async-done(((bf16[16,32,128]{2,0,1:T(8,128)(2,1)}), bf16[256,32,128]{2,0,1:T(8,128)(2,1)}) %all-gather.6.cloned.1.call-update) | async-done | bytes 2097168 | tf_op jit(solution)/shard_map/all_gather | solution.py:154
  124.8 3.6 %fusion.4 = f32[16,32,512,1]{2,1,3,0:T(8,128)S(1)} fusion(bf16[16,128,512,1]{2,1,0,3:T(8,128)(2,1)} %bitcast.172, bf16[16,16,32,128]{3,1,0,2:T(8,128)(2,1)} %bitcast.173), kind=kOutput, calls=%fused_computation.4 | convolution fusion | flops 1073741824 | bytes 5242880 | tf_op jit(solution)/shard_map/pmi,cpom->ico/dot_general | solution.py:182
  128.3 1.3 copy.79
  (43 shorter events, 0.6 us)
Async XLA Ops:
  7.2 32.7 %copy-start = (f32[3,512]{1,0:T(4,128)S(1)}, f32[3,512]{1,0:T(4,128)}, u32[]{:S(2)}) copy-start(f32[3,512]{1,0:T(4,128)} %param.15) | copy-start | bytes 18436
  12.5 8.7 %copy-start.3 = (bf16[128,512]{1,0:T(8,128)(2,1)S(1)}, bf16[128,512]{1,0:T(8,128)(2,1)}, u32[]{:S(2)}) copy-start(bf16[128,512]{1,0:T(8,128)(2,1)} %param.11) | copy-start | bytes 393220
  13.5 26.7 %all-to-all-start = ((bf16[6,16,32,128]{3,2,0,1:T(8,128)(2,1)}), bf16[6,16,32,128]{3,2,0,1:T(8,128)(2,1)S(1)}, u32[]{:S(2)}, u32[]{:S(2)}) async-start(bf16[6,16,32,128]{3,2,0,1:T(8,128)(2,1)} %copy.56), calls=%async_computation | async-start | bytes 1572864 | tf_op jit(solution)/shard_map/all_to_all | solution.py:120
  21.1 79.0 %all-gather.4.cloned.1.call-start = ((), (), s32[]{:S(2)}) async-start(), calls=%async_computation.2 | async-start | bytes 2621440 | tf_op jit(solution)/shard_map/all_gather | solution.py:116
  39.8 85.0 %all-gather.6.cloned.1.call-start = ((), (), s32[]{:S(2)}) async-start(), calls=%async_computation.3 | async-start | bytes 2228224 | tf_op jit(solution)/shard_map/all_gather | solution.py:154
  40.2 0.7 copy-start.7
  40.5 2.3 %copy-start.1 = (f32[32,128]{1,0:T(8,128)S(1)}, f32[32,128]{1,0:T(8,128)}, u32[]{:S(2)}) copy-start(f32[32,128]{1,0:T(8,128)} %constant.65) | copy-start | bytes 49156
  40.5 2.3 %copy-start.2 = (f32[32,128]{1,0:T(8,128)S(1)}, f32[32,128]{1,0:T(8,128)}, u32[]{:S(2)}) copy-start(f32[32,128]{1,0:T(8,128)} %constant.64) | copy-start | bytes 49156
  49.9 0.7 copy-start.6
  53.5 4.7 %copy-start.5 = (f32[64,16,1]{0,1,2:T(8,128)S(1)}, f32[64,16,1]{0,1,2:T(8,128)}, u32[]{:S(2)}) copy-start(f32[64,16,1]{0,1,2:T(8,128)} %constant.69) | copy-start | bytes 12292
  54.0 8.3 %collective-permute-start = (bf16[16,32,128]{2,0,1:T(8,128)(2,1)S(1)}, bf16[16,32,128]{2,0,1:T(8,128)(2,1)}, u32[]{:S(2)}, u32[]{:S(2)}) collective-permute-start(bf16[16,32,128]{2,0,1:T(8,128)(2,1)S(1)} %get-tuple-element.17), channel_id=1, source_target_pairs={{0,0},{1,16},{2,32},{3,48},{4,64},{5,80},{6,96},{7,112},{8,128},{9... | collective-permute-start | bytes 393224 | tf_op jit(solution)/shard_map/ppermute | solution.py:153
  67.0 0.7 copy-start.4
Sparse Core Ops, SparseCore 0:
  39.9 38.9 all-gather.3
  80.6 44.1 all-gather.5

commit v7 on v6

--- a/solution.py
+++ b/solution.py
@@ -8,7 +8,7 @@
 
 F32 = jnp.float32
 BF16 = jnp.bfloat16
-PRECISE = lax.Precision.HIGHEST
+PRECISE = lax.Precision.HIGH
 SEQ = ("y", "x")
 SEQ_NAME, CHAN_NAME = "seq", "chan"
 CHAN = ("z", "core")
@@ -169,13 +169,14 @@
     width = value_t.shape[2]
     taps_slab = jnp.pad(jnp.concatenate([taps_high, taps_low], axis=0).T, ((0, 0), (0, width - 2 * tap_count)))
     taps_slab = jnp.broadcast_to(taps_slab[None], value_t.shape)
-    outs = jnp.stack([grad_gate, grad_key, grad_value, grad_filter.astype(BF16), taps_slab])
+    gf_high, gf_low = split_words(grad_filter)
+    outs = jnp.stack([grad_gate, grad_key, grad_value, gf_high, gf_low, taps_slab])
     outs = lax.all_to_all(outs, SEQ, split_axis=1, concat_axis=1, tiled=True)
-    taps_got = outs[4, :, :, : 2 * tap_count]
+    taps_got = outs[5, :, :, : 2 * tap_count]
     grad_taps = join_words(taps_got[..., :tap_count], taps_got[..., tap_count:])
     grad_taps = jnp.transpose(grad_taps, (2, 0, 1)).reshape(tap_count, -1)
-    outs = from_tokens_in_lanes(outs[:4])
-    grad_filter = outs[3].astype(F32)
+    outs = from_tokens_in_lanes(outs[:5])
+    grad_filter = join_words(outs[3], outs[4])
 
     blocks = value_t.shape[0]
     inputs_3 = inputs_all.reshape(blocks, width, inputs_all.shape[1])

time: 137 us -> 137 us (level)
  matrix products: 22.6 us -> 16.5 us
  waiting for transfers between devices: 24.7 us -> 27.1 us
  local copies, waits for them, and re-layouts: 14.3 us -> 16.3 us
    all_gather x1, waiting for transfers between devices: 24.7 us -> 27.1 us  [on_device(): value_cols = lax.all_gather(value_swapped, CHAN, axis=0, tiled=False)]
    unnamed x34 -> x53, local copies, waits for them, and re-layouts: 10.6 us -> 11.8 us
  transfers between devices with their start and end apart: 4 -> 4, of which waited for: 1 -> 1; matrix products, arithmetic and copies ran while one was open for 21% -> 18% of each run, Pallas kernels for 0% -> 0%
where the time goes in v7:
time: 137 us
  blocking collectives  46.1 us (34%)
  waiting for transfers between devices  27.1 us (20%)
  matrix products  16.5 us (12%)
  local copies, waits for them, and re-layouts  16.3 us (12%)
  between operations  14.8 us (11%)
  starting transfers between devices  12.1 us (9%)
  other arithmetic  3.75 us (3%)
    all_to_all x1, blocking collectives, on_device(): outs = lax.all_to_all(outs, SEQ, split_axis=1, concat_axis=1, tiled=True)  27.6 us
    all_gather x1, waiting for transfers between devices, on_device(): value_cols = lax.all_gather(value_swapped, CHAN, axis=0, tiled=False)  27.1 us
    all_gather x1, blocking collectives, on_device(): inputs_all = lax.all_gather(layer_input, 'x', axis=0, tiled=True)  18.5 us
    unnamed x53, local copies, waits for them, and re-layouts  11.8 us
    all_to_all x1, starting transfers between devices, on_device(): got = lax.all_to_all(sent, SEQ, split_axis=1, concat_axis=1, tiled=True)  7.57 us
    ppermute x1, starting transfers between devices, on_device(): value_swapped = lax.ppermute(grad_value, SEQ + CHAN, swap)  4.42 us
    dot_general x1, matrix products, on_device(): jnp.einsum('pmi,cpom->ico', inputs_3, value_cols, preferred_element_type=...  3.58 us
    dot_general x2, matrix products, signals_back(): return jnp.einsum('pk,kscm->pscm', back_a, both, precision=PRECISE)  3 us
  transfers between devices with their start and end apart: 4, of which 1 were waited for; matrix products, arithmetic and copies ran while one was open for 18% of the time, Pallas kernels for 0%

profile of v7, /device:TPU:1, one launch (start us, length us, event | category | flops | bytes accessed | tf_op | source)
XLA Modules:
  0.0 136.6 jit_solution(8261989198121097290)
XLA Ops:
  7.2 1.0 copy.50
  8.2 1.0 copy.51
  9.3 1.0 copy.52
  10.3 1.0 copy.53
  11.3 1.1 copy.54
  12.5 0.1 fusion.45
  12.6 1.0 copy.56
  13.5 7.6 %all-to-all-start = ((bf16[6,16,32,128]{3,2,0,1:T(8,128)(2,1)}), bf16[6,16,32,128]{3,2,0,1:T(8,128)(2,1)S(1)}, u32[]{:S(2)}, u32[]{:S(2)}) async-start(bf16[6,16,32,128]{3,2,0,1:T(8,128)(2,1)} %copy.56), calls=%async_computation | async-start | bytes 1572864 | tf_op jit(solution)/shard_map/all_to_all | solution.py:120
  21.2 18.5 %all_gather.14 = bf16[512,512]{1,0:T(8,128)(2,1)} all-gather(bf16[128,512]{1,0:T(8,128)(2,1)S(1)} %copy-done.13), channel_id=1, replica_groups=mesh['y'=4,'x'=4,'z'=8,'core'=2] {'x'}, dimensions={0}, use_global_device_ids=true | all-gather | bytes 655360 | tf_op jit(solution)/shard_map/all_gather | solution.py:115
  39.9 0.1 constant_dynamic-slice_fusion
  40.0 0.2 fusion.76
  40.2 0.1 fusion.86
  40.3 0.1 copy_convert_fusion
  40.4 0.1 pad_slice_fusion.3
  40.6 0.1 slice.256
  40.7 0.1 slice.258
  40.9 0.1 pad_slice_fusion.1
  41.1 0.2 fusion.32
  41.2 1.0 fusion.16
  42.3 0.3 multiply_subtract_fusion.1
  42.6 1.3 fusion.14
  44.0 1.4 %convolution_add_fusion.1 = f32[32,2,32,256]{3,2,1,0:T(8,128)S(1)} fusion(f32[32,2,32,256]{3,2,1,0:T(8,128)S(1)} %fusion.14, f32[32,2,32,128]{3,0,2,1:T(8,128)S(1)} %get-tuple-element.44, f32[128,128]{1,0:T(8,128)S(1)} %get-tuple-element.73, f32[128,128]{1,0:T(8,128)S(1)} %get-tuple-element.72), kind=kOutput, calls=%fused_computation.7 | convolution fusion | flops 403210240 | bytes 5373952 | tf_op jit(solution)/shard_map/kscm,mn->kscn/dot_general | solution.py:57
  45.4 0.6 fusion.21
  45.9 0.6 fusion.7
  46.5 0.2 multiply_subtract_fusion.5
  46.7 0.1 maximum_bitcast_fusion
  46.8 0.4 copy-done.16
  47.2 2.3 %multiply_reduce_fusion.2 = (f32[32]{0:T(128)S(1)}, f32[32]{0:T(128)S(1)}, f32[32]{0:T(128)S(1)}, f32[16,32,128]{2,0,1:T(8,128)S(1)}, f32[16,32,128]{2,0,1:T(8,1...) fusion(bf16[1,16,32,128]{3,2,0,1:T(8,128)(2,1)S(1)} %get-tuple-element.65, ...), kind=kOutput, calls=%fused_computation.79 | convolution fusion | flops 26148768 | bytes 3412608 | tf_op jit(solution)/shard_map/pk,kscm->pscm/dot_general | solution.py:73
  49.5 0.1 slice.252
  49.7 0.1 slice.250
  49.8 0.1 pad_slice_fusion.5
  50.0 0.1 pad_slice_fusion.7
  50.1 0.1 copy-done.1
  50.2 1.2 convert_multiply_fusion
  51.4 1.2 fusion.85
  52.6 0.1 copy.99
  52.7 4.4 %collective-permute-start = (bf16[16,32,128]{2,0,1:T(8,128)(2,1)}, bf16[16,32,128]{2,0,1:T(8,128)(2,1)}, u32[]{:S(2)}, u32[]{:S(2)}) collective-permute-start(bf16[16,32,128]{2,0,1:T(8,128)(2,1)} %get-tuple-element.17), channel_id=1, source_target_pairs={{0,0},{1,16},{2,32},{3,48},{4,64},{5,80},{6,96},{7,112},{8,128},{9... | collective-permute-start | bytes 393224 | tf_op jit(solution)/shard_map/ppermute | solution.py:153
  57.2 0.6 fusion.87
  57.8 0.1 multiply_subtract_fusion.4
  58.0 0.7 fusion.24
  58.7 0.7 fusion.6
  59.5 0.4 multiply_add_fusion.2
  59.9 0.1 pad_maximum_fusion
  59.9 1.5 %fusion.9 = f32[32,2,32,256]{3,0,2,1:T(8,128)S(1)} fusion(f32[32,2,32,128]{3,2,1,0:T(8,128)S(1)} %pad_maximum_fusion, f32[128,128]{1,0:T(8,128)S(1)} %get-tuple-element.73, f32[128,128]{1,0:T(8,128)S(1)} %get-tuple-element.72), kind=kOutput, calls=%fused_computation.16 | convolution fusion | flops 402685952 | bytes 3276800 | tf_op jit(solution)/shard_map/kscn,nm->kscm/dot_general | solution.py:66
  61.4 0.1 pad_maximum_fusion.1
  61.5 1.5 %convolution_add_fusion = f32[32,2,32,256]{3,0,2,1:T(8,128)S(1)} fusion(f32[32,2,32,256]{3,0,2,1:T(8,128)S(1)} %fusion.9, f32[32,2,32,128]{3,2,1,0:T(8,128)S(1)} %pad_maximum_fusion.1, f32[128,128]{1,0:T(8,128)S(1)} %get-tuple-element.73, f32[128,128]{1,0:T(8,128)S(1)} %get-tuple-element.71), kind=kOutput, calls=%fused_computation.6 | convolution fusion | flops 403210240 | bytes 5373952 | tf_op jit(solution)/shard_map/kscn,nm->kscm/dot_general | solution.py:66
  63.0 0.3 multiply_subtract_fusion
  63.4 0.3 copy-done.14
  63.7 0.7 fusion
  64.4 0.1 fusion.46
  64.5 0.2 fusion.42
  64.7 0.9 bitcast_dynamic-update-slice_fusion
  65.8 0.2 copy.71
  66.0 27.6 %all_to_all.10 = bf16[6,16,32,128]{3,2,0,1:T(8,128)(2,1)S(1)} all-to-all(bf16[6,16,32,128]{3,2,0,1:T(8,128)(2,1)S(1)} %copy.71), channel_id=1, replica_groups=mesh['y'=4,'x'=4,'z'=8,'core'=2] {'y','x'}, dimensions={1} | all-to-all | bytes 1572864 | tf_op jit(solution)/shard_map/all_to_all | solution.py:174
  93.6 0.1 copy.98
  93.7 0.8 copy.75
  94.5 0.8 copy.76
  95.3 0.8 copy.77
  96.1 0.1 convert_add_fusion
  96.2 0.7 copy.91
  96.9 0.8 copy.78
  97.8 27.1 %all-gather.6.cloned.1.call-done = bf16[256,32,128]{2,0,1:T(8,128)(2,1)} async-done(((bf16[16,32,128]{2,0,1:T(8,128)(2,1)}), bf16[256,32,128]{2,0,1:T(8,128)(2,1)}) %all-gather.6.cloned.1.call-update) | async-done | bytes 2097168 | tf_op jit(solution)/shard_map/all_gather | solution.py:154
  124.8 3.6 %fusion.4 = f32[16,32,512,1]{2,1,3,0:T(8,128)S(1)} fusion(bf16[16,128,512,1]{2,1,0,3:T(8,128)(2,1)} %bitcast.176, bf16[16,16,32,128]{3,1,0,2:T(8,128)(2,1)} %bitcast.177), kind=kOutput, calls=%fused_computation.4 | convolution fusion | flops 1073741824 | bytes 5242880 | tf_op jit(solution)/shard_map/pmi,cpom->ico/dot_general | solution.py:183
  128.4 1.3 copy.79
  (65 shorter events, 0.8 us)
Async XLA Ops:
  7.2 32.7 %copy-start = (f32[3,512]{1,0:T(4,128)S(1)}, f32[3,512]{1,0:T(4,128)}, u32[]{:S(2)}) copy-start(f32[3,512]{1,0:T(4,128)} %param.15) | copy-start | bytes 18436
  12.5 8.7 %copy-start.13 = (bf16[128,512]{1,0:T(8,128)(2,1)S(1)}, bf16[128,512]{1,0:T(8,128)(2,1)}, u32[]{:S(2)}) copy-start(bf16[128,512]{1,0:T(8,128)(2,1)} %param.11) | copy-start | bytes 393220
  13.5 26.7 %all-to-all-start = ((bf16[6,16,32,128]{3,2,0,1:T(8,128)(2,1)}), bf16[6,16,32,128]{3,2,0,1:T(8,128)(2,1)S(1)}, u32[]{:S(2)}, u32[]{:S(2)}) async-start(bf16[6,16,32,128]{3,2,0,1:T(8,128)(2,1)} %copy.56), calls=%async_computation | async-start | bytes 1572864 | tf_op jit(solution)/shard_map/all_to_all | solution.py:120
  21.1 76.6 %all-gather.4.cloned.1.call-start = ((), (), s32[]{:S(2)}) async-start(), calls=%async_computation.2 | async-start | bytes 2621440 | tf_op jit(solution)/shard_map/all_gather | solution.py:116
  39.8 85.1 %all-gather.6.cloned.1.call-start = ((), (), s32[]{:S(2)}) async-start(), calls=%async_computation.3 | async-start | bytes 2228224 | tf_op jit(solution)/shard_map/all_gather | solution.py:154
  40.3 0.8 copy-start.8
  40.4 0.8 copy-start.17
  40.9 1.4 %copy-start.11 = (f32[32,128]{1,0:T(8,128)S(1)}, f32[32,128]{1,0:T(8,128)}, u32[]{:S(2)}) copy-start(f32[32,128]{1,0:T(8,128)} %constant.65) | copy-start | bytes 49156
  40.9 1.4 %copy-start.12 = (f32[32,128]{1,0:T(8,128)S(1)}, f32[32,128]{1,0:T(8,128)}, u32[]{:S(2)}) copy-start(f32[32,128]{1,0:T(8,128)} %constant.64) | copy-start | bytes 49156
  46.5 0.7 copy-start.16
  49.5 0.7 copy-start.1
  49.5 1.9 %copy-start.3 = (f32[16,32,128]{2,0,1:T(8,128)}, f32[16,32,128]{2,0,1:T(8,128)S(1)}, u32[]{:S(2)}) copy-start(f32[16,32,128]{2,0,1:T(8,128)S(1)} %get-tuple-element.40) | copy-start | bytes 786436
  51.4 5.8 %copy-start.15 = (f32[64,16,1]{0,1,2:T(8,128)S(1)}, f32[64,16,1]{0,1,2:T(8,128)}, u32[]{:S(2)}) copy-start(f32[64,16,1]{0,1,2:T(8,128)} %constant.69) | copy-start | bytes 12292
  52.7 8.8 %collective-permute-start = (bf16[16,32,128]{2,0,1:T(8,128)(2,1)}, bf16[16,32,128]{2,0,1:T(8,128)(2,1)}, u32[]{:S(2)}, u32[]{:S(2)}) collective-permute-start(bf16[16,32,128]{2,0,1:T(8,128)(2,1)} %get-tuple-element.17), channel_id=1, source_target_pairs={{0,0},{1,16},{2,32},{3,48},{4,64},{5,80},{6,96},{7,112},{8,128},{9... | collective-permute-start | bytes 393224 | tf_op jit(solution)/shard_map/ppermute | solution.py:153
  57.9 1.5 %copy-start.5 = (f32[32,1,32,128]{3,2,1,0:T(8,128)S(1)}, f32[32,1,32,128]{3,2,1,0:T(8,128)}, u32[]{:S(2)}) copy-start(f32[32,1,32,128]{3,2,1,0:T(8,128)} %get-tuple-element.14) | copy-start | bytes 1572868
  57.9 1.5 %copy-start.6 = (f32[32,1,32,128]{3,2,1,0:T(8,128)S(1)}, f32[32,1,32,128]{3,2,1,0:T(8,128)}, u32[]{:S(2)}) copy-start(f32[32,1,32,128]{3,2,1,0:T(8,128)} %get-tuple-element.15) | copy-start | bytes 1572868
  57.9 1.5 %copy-start.7 = (f32[32,1,32,128]{3,2,1,0:T(8,128)S(1)}, f32[32,1,32,128]{3,2,1,0:T(8,128)}, u32[]{:S(2)}) copy-start(f32[32,1,32,128]{3,2,1,0:T(8,128)} %get-tuple-element.12) | copy-start | bytes 1572868
  63.0 0.7 copy-start.14
  63.3 1.1 copy-start.9
  63.3 1.1 copy-start.2
  63.4 1.1 copy-start.4
  63.4 1.2 copy-start.10
Sparse Core Ops, SparseCore 0:
  39.9 39.1 all-gather.3
  80.8 43.9 all-gather.5
